TPU v7x, 32 devices: a whole 2x2x4 slice. The times are simulated.
32 devices in a mesh: parts: 2 (over y), row: 4 (over x, core), col: 4 (over z).
Axes of the slice: x: 2, y: 2, z: 4, core: 2. Of those that a mesh axis runs over, the one named last changes fastest.
Arguments:
- basis: float32 [2048, 16384], P(('parts', 'row'), 'col'), parts along dimension 0, may hold values from -6 to 6
- panel_one: float32 [32768, 256], P(('parts', 'col', 'row')), parts along dimension 0, may hold values from -192 to 192
- panel_two: float32 [32768, 256], P(('parts', 'col', 'row')), parts along dimension 0, may hold values from -192 to 192
- gradient: float32 [2048, 512], P(('parts', 'row')), parts along dimension 0, may hold values from -0.25 to 0.25
Outputs:
- new_basis: float32 [2048, 16384], P(('parts', 'row'), 'col'), parts along dimension 0
- rotated: float32 [1024, 16384], P(('parts', 'row'), 'col'), parts along dimension 0
There are 2 independent parts, one for each index of `parts`. A program takes and returns all parts, laid end to end along the dimension named above; each array names one. Nothing has to cross between parts.
All inputs are finite; a program needn't handle non-finite values.
Results may differ from a plain program's by a relative error of at most 0.0001.
Values sent between devices are 32-bit elements; how exact they have to be, the bound alone decides.
No kernel may reach another device: no remote copies, remote signals or barrier semaphores. Data moves between devices by JAX's collectives and lax.ppermute only.
A program may use at most 64 MiB of HBM per device.

v0:
```python
import jax
import jax.numpy as jnp
from jax import lax
from jax.sharding import PartitionSpec as P


def dot_high(left, right):
    return jnp.dot(left, right, precision=lax.Precision.HIGHEST, preferred_element_type=jnp.float32)


def inner_rows(left, right):
    return jnp.einsum(
        "ra,rb->ab",
        left,
        right,
        precision=lax.Precision.HIGHEST,
        preferred_element_type=jnp.float32,
    )


def outer_cols(left, right):
    return jnp.einsum(
        "rk,ck->rc",
        left,
        right,
        precision=lax.Precision.HIGHEST,
        preferred_element_type=jnp.float32,
    )


def outer_mid(left, right):
    return jnp.einsum(
        "rk,ck->rc",
        left,
        right,
        precision=lax.Precision.HIGH,
        preferred_element_type=jnp.float32,
    )


def inner_mid(left, right):
    return jnp.einsum(
        "ra,rb->ab",
        left,
        right,
        precision=lax.Precision.HIGH,
        preferred_element_type=jnp.float32,
    )


def tri_inverse(upper):
    size = upper.shape[0]
    width = 8
    count = size // width
    shaped = upper.reshape(count, width, count, width)
    selector = jnp.eye(count, dtype=upper.dtype)
    blocks = jnp.einsum("iajb,ij->iab", shaped, selector, precision=lax.Precision.HIGHEST)
    inverse = jnp.zeros_like(blocks)
    unit = jnp.eye(width, dtype=upper.dtype)
    for line in range(width - 1, -1, -1):
        known = jnp.einsum(
            "bj,bjc->bc", blocks[:, line, :], inverse, precision=lax.Precision.HIGHEST
        )
        value = (unit[line][None, :] - known) / blocks[:, line, line][:, None]
        inverse = inverse.at[:, line, :].set(value)
    span = width
    while count > 1:
        shaped = upper.reshape(count, span, count, span)
        pairs = count // 2
        lefts = jnp.arange(pairs) * 2
        pick = (
            (jnp.arange(count)[None, :, None] == lefts[:, None, None])
            & (jnp.arange(count)[None, None, :] == lefts[:, None, None] + 1)
        ).astype(upper.dtype)
        corner = jnp.einsum("iajb,pij->pab", shaped, pick, precision=lax.Precision.HIGHEST)
        first = inverse[0::2]
        second = inverse[1::2]
        top = -jnp.einsum(
            "pab,pbc->pac",
            jnp.einsum("pab,pbc->pac", first, corner, precision=lax.Precision.HIGHEST),
            second,
            precision=lax.Precision.HIGHEST,
        )
        upper_half = jnp.concatenate([first, top], axis=2)
        lower_half = jnp.concatenate([jnp.zeros_like(second), second], axis=2)
        inverse = jnp.concatenate([upper_half, lower_half], axis=1)
        count = pairs
        span = span * 2
    return inverse[0]


def tri_factor(gram):
    upper = jnp.triu(gram, 1) + jnp.diag(jnp.diag(gram)) * 0.5
    return tri_inverse(upper)


def tri_factor_doubling(gram):
    size = gram.shape[0]
    upper = jnp.triu(gram, 1) + jnp.diag(jnp.diag(gram)) * 0.5
    index = jnp.arange(size)
    same = index[:, None] == index[None, :]
    inverse = jnp.where(same, 1.0 / jnp.diag(upper)[None, :], 0.0)
    span = 1
    while span < size:
        group = index // (2 * span)
        side = (index // span) % 2
        corner = (group[:, None] == group[None, :]) & (side[:, None] == 0) & (side[None, :] == 1)
        inverse = inverse - dot_high(dot_high(inverse, jnp.where(corner, upper, 0.0)), inverse)
        span *= 2
    return inverse


def swap(value, distance, size):
    return lax.ppermute(value, "row", [(i, i ^ distance) for i in range(size)])


def spread(size):
    steps = []
    distance = 1
    while distance < size:
        steps.append(distance)
        distance *= 2
    return steps


def slot_order(me, size):
    steps = spread(size)
    order = []
    for slot in range(size):
        mask = 0
        for level, distance in enumerate(steps):
            if not (slot >> (len(steps) - 1 - level)) & 1:
                mask ^= distance
        order.append(mask)
    return jnp.array(order) ^ me


def col_sum(value):
    size = lax.axis_size("col")
    for distance in spread(size):
        value = value + lax.ppermute(
            value, "col", [(i, i ^ distance) for i in range(size)]
        )
    return value


def scatter_rows(value, size):
    for distance in spread(size):
        count = value.shape[0] // 2
        value = value[count:] + swap(value[:count], distance, size)
    return value


def shards(basis, panel_one, panel_two, gradient):
    size = lax.axis_size("row")
    k = panel_one.shape[1]
    span = panel_one.shape[0]
    lanes = gradient.shape[1] // size
    me = lax.axis_index("row")
    own = jnp.concatenate([panel_one, panel_two], axis=1)
    held = {0: own}
    beside = swap(own, 1, size)
    landed = own
    for distance in reversed(spread(size)):
        keys = [key for key in sorted(held) if distance > 1 or key]
        if distance == 1:
            held[1] = beside
        if keys:
            got = swap(jnp.stack([held[key] for key in keys]), distance, size)
            if distance > 1:
                landed = got
            for index, key in enumerate(keys):
                held[key ^ distance] = got[index]
    held = jnp.stack([held[key] for key in range(size)])

    order = slot_order(me, size)
    shuffled = jnp.take(gradient.reshape(-1, size, lanes), order, axis=1).reshape(gradient.shape)
    head = inner_mid(shuffled, basis)
    count = head.shape[0] // 2
    head = head[count:] + swap(head[:count], 1, size)

    gram_own = inner_rows(own, own)
    gram_chip = gram_own + swap(gram_own, 1, size)
    half = me % 2
    rows = gram_chip.shape[0] // 2
    mine = col_sum(lax.dynamic_slice_in_dim(gram_chip, half * rows, rows, axis=0))
    mine, head = lax.optimization_barrier((mine, head))
    for distance in spread(size)[1:]:
        mine = mine + swap(mine, distance, size)
    halves = jnp.stack([mine, swap(mine, 1, size)])
    gram = jnp.take(halves, jnp.array([0, 1]) ^ half, axis=0).reshape(2 * rows, -1)

    head, _ = lax.optimization_barrier((head, landed))
    for distance in spread(size)[1:]:
        count = head.shape[0] // 2
        head = head[count:] + swap(head[:count], distance, size)

    image = None
    for slot in range(size):
        cols = lax.dynamic_slice_in_dim(basis, (me ^ slot) * span, span, axis=1)
        part = dot_high(cols, held[slot])
        image = part if image is None else image + part
    image = col_sum(image)

    gathered = jnp.take(held, jnp.arange(size) ^ me, axis=0).reshape(size * span, -1)
    factor_one = tri_factor_doubling(gram[:k, :k])
    factor_two = tri_factor_doubling(gram[k:, k:])
    first = dot_high(image[:, :k], factor_one)
    image_two = image[:, k:] - dot_high(first, gram[:k, k:])
    second = dot_high(image_two, factor_two)
    weight = jnp.concatenate([first, second], axis=1)
    new_basis = basis - outer_mid(weight, gathered)
    tail = scatter_rows(inner_rows(shuffled, weight), size)
    rotated = head - outer_mid(tail, gathered)
    return (new_basis, rotated)


def solution(mesh):
    return jax.shard_map(
        shards,
        mesh=mesh,
        in_specs=(
            P(("parts", "row"), "col"),
            P(("parts", "col", "row"), None),
            P(("parts", "col", "row"), None),
            P(("parts", "row"), None),
        ),
        out_specs=(P(("parts", "row"), "col"), P(("parts", "row"), "col")),
        check_vma=False,
    )
```

profile of v0, /device:TPU:0, one launch (start us, length us, event | category | flops | bytes accessed | tf_op | source)
XLA Modules:
  0.0 169.4 jit_solution(8451384037710983106)
XLA Ops:
  3.8 6.2 %fusion.181 = f32[512,4096]{1,0:T(8,128)S(1)} fusion(f32[256,512]{0,1:T(8,128)S(1)} %bitcast_select_fusion.2, f32[256,4096]{1,0:T(8,128)} %param.6), kind=kOutput, calls=%fused_computation.307 | convolution fusion | flops 3221225472 | bytes 13107200 | tf_op jit(solution)/shard_map/ra,rb->ab/dot_general | solution.py:42
  10.0 2.5 %slice.68 = f32[256,4096]{1,0:T(8,128)} slice(f32[512,4096]{1,0:T(8,128)S(1)} %fusion.181), slice={[0:256], [0:4096]} | slice | bytes 8388608 | tf_op jit(solution)/shard_map/slice | solution.py:180
  12.4 2.3 %copy-done = f32[512,4096]{1,0:T(8,128)} copy-done((f32[512,4096]{1,0:T(8,128)}, f32[512,4096]{1,0:T(8,128)S(1)}, u32[]{:S(2)}) %copy-start) | copy-done | bytes 8388632
  15.6 3.0 %collective-permute-start.1 = (f32[1,1024,512]{2,1,0:T(8,128)S(1)}, f32[1,1024,512]{2,1,0:T(8,128)}, u32[]{:S(2)}, u32[]{:S(2)}) collective-permute-start(f32[1,1024,512]{2,1,0:T(8,128)S(1)} %bitcast.92), channel_id=1, source_target_pairs={{0,8},{4,12},{8,0},{12,4},{1,9},{5,13},{9,1},{13,5},{2,10},{6,14},... | collective-permute-start | bytes 6291464 | tf_op jit(solution)/shard_map/ppermute | solution.py:114
  18.6 4.6 %fusion.180 = f32[512,512]{1,0:T(8,128)} fusion(f32[1024,512]{1,0:T(8,128)S(1)} %constant_dynamic-update-slice_fusion), kind=kOutput, calls=%fused_computation.306 | convolution fusion | flops 3221225472 | bytes 3145728 | tf_op jit(solution)/shard_map/ra,rb->ab/dot_general | solution.py:12
  23.4 3.5 %collective-permute-done.5 = f32[512,512]{1,0:T(8,128)} collective-permute-done((f32[512,512]{1,0:T(8,128)}, f32[512,512]{1,0:T(8,128)}, u32[]{:S(2)}, u32[]{:S(2)}) %collective-permute-start.5) | collective-permute-done | bytes 1048608 | tf_op jit(solution)/shard_map/ppermute | solution.py:114
  28.1 3.0 %collective-permute-start.6 = (f32[256,512]{1,0:T(8,128)S(1)}, f32[256,512]{1,0:T(8,128)S(1)}, u32[]{:S(2)}, u32[]{:S(2)}) collective-permute-start(f32[256,512]{1,0:T(8,128)S(1)} %dynamic-slice_add_fusion), channel_id=1, source_target_pairs={{0,1},{1,0},{2,3},{3,2},{4,5},{5,4},{6,7},{7,6},{8,9},{9,8},{10,11... | collective-permute-start | bytes 1572872 | tf_op jit(solution)/shard_map/ppermute | solution.py:141
  31.2 12.1 %collective-permute-done.6 = f32[256,512]{1,0:T(8,128)S(1)} collective-permute-done((f32[256,512]{1,0:T(8,128)S(1)}, f32[256,512]{1,0:T(8,128)S(1)}, u32[]{:S(2)}, u32[]{:S(2)}) %collective-permute-start.6) | collective-permute-done | bytes 524320 | tf_op jit(solution)/shard_map/ppermute | solution.py:141
  43.5 2.8 %collective-permute-start.7 = (f32[256,512]{1,0:T(8,128)S(1)}, f32[256,512]{1,0:T(8,128)}, u32[]{:S(2)}, u32[]{:S(2)}) collective-permute-start(f32[256,512]{1,0:T(8,128)S(1)} %add.359), channel_id=1, source_target_pairs={{0,2},{1,3},{2,0},{3,1},{4,6},{5,7},{6,4},{7,5},{8,10},{9,11},{10,... | collective-permute-start | bytes 1572872 | tf_op jit(solution)/shard_map/ppermute | solution.py:141
  46.4 18.2 %collective-permute-done.1 = f32[1,1024,512]{2,1,0:T(8,128)} collective-permute-done((f32[1,1024,512]{2,1,0:T(8,128)S(1)}, f32[1,1024,512]{2,1,0:T(8,128)}, u32[]{:S(2)}, u32[]{:S(2)}) %collective-permute-start.1) | collective-permute-done | bytes 2097184 | tf_op jit(solution)/shard_map/ppermute | solution.py:114
  64.6 3.2 %fusion.13 = f32[256,512]{1,0:T(8,128)S(1)} fusion(f32[1024,512]{1,0:T(8,128)S(1)} %constant_dynamic-update-slice_fusion, f32[256,4096]{1,0:T(8,128)} %param.6, s32[]{:T(128)S(6)} %select_n.477), kind=kOutput, calls=%fused_computation.40 | convolution fusion | flops 1610612736 | bytes 3670020 | tf_op jit(solution)/shard_map/dot_general | solution.py:8
  67.8 1.5 collective-permute-done.7
  70.4 3.5 %convolution_add_fusion = f32[256,512]{1,0:T(8,128)S(1)} fusion(f32[256,512]{1,0:T(8,128)S(1)} %fusion.13, f32[1024,512]{1,0:T(8,128)} %collective-permute-done, f32[256,4096]{1,0:T(8,128)S(1)} %copy-done.1, s32[]{:T(128)S(6)} %select_n.478), kind=kOutput, calls=%fused_computation.18 | convolution fusion | flops 1610743808 | bytes 4194308 | tf_op jit(solution)/shard_map/dot_general | solution.py:8
  74.0 3.9 %slice_add_fusion = f32[256,4096]{1,0:T(8,128)S(1)} fusion(f32[256,4096]{1,0:T(8,128)} %collective-permute-done.8, f32[512,4096]{1,0:T(8,128)} %copy-done), kind=kLoop, calls=%fused_computation.10 | loop fusion | flops 1048576 | bytes 12582912 | tf_op jit(solution)/shard_map/add | solution.py:180
  77.9 1.4 collective-permute-start.9
  79.4 3.5 %fusion.4 = f32[256,512]{1,0:T(8,128)S(1)} fusion(f32[256,512]{1,0:T(8,128)S(1)} %convolution_add_fusion, f32[1,1024,512]{2,1,0:T(8,128)} %collective-permute-done.1, f32[256,4096]{1,0:T(8,128)S(1)} %copy-done.1, s32[]{:T(128)S(6)} %select_n.479), kind=kOutput, calls=%fused_computation.16 | convolution fusion | flops 1610743808 | bytes 4194308 | tf_op jit(solution)/shard_map/dot_general | solution.py:8
  82.9 2.1 %fusion.7 = f32[256,512]{1,0:T(8,128)S(1)} fusion(f32[256,512]{1,0:T(8,128)S(1)} %fusion.4, f32[1,1024,512]{2,1,0:T(8,128)S(1)} %collective-permute-done.2, f32[256,4096]{1,0:T(8,128)S(1)} %copy-done.1, s32[]{:T(128)S(6)} %select_n.480), kind=kOutput, calls=%fused_computation.17 | convolution fusion | flops 1610743808 | bytes 4194308 | tf_op jit(solution)/shard_map/dot_general | solution.py:8
  85.7 5.2 %collective-permute-done.9 = f32[256,512]{1,0:T(8,128)S(1)} collective-permute-done((f32[256,512]{1,0:T(8,128)S(1)}, f32[256,512]{1,0:T(8,128)S(1)}, u32[]{:S(2)}, u32[]{:S(2)}) %collective-permute-start.9) | collective-permute-done | bytes 524320 | tf_op jit(solution)/shard_map/ppermute | solution.py:114
  91.8 1.5 slice.47
  93.3 1.7 collective-permute-start.11
  95.0 5.5 %pad_maximum_fusion = f32[4,1024,512]{2,1,0:T(8,128)} fusion(f32[1,1024,512]{2,1,0:T(8,128)S(1)} %collective-permute-done.2, f32[1,1024,512]{2,1,0:T(8,128)} %collective-permute-done.1, f32[1,1024,512]{2,1,0:T(8,128)} %bitcast.11, f32[1,1024,512]{2,1,0:T(8,128)S(1)} %bitcast.93), kind=kLoop, calls=%fused_computation.7 | loop fusion | flops 6291456 | bytes 16777216 | tf_op jit(solution)/shard_map/stack | solution.py:174
  100.4 7.7 %gather_fusion.6 = f32[4,1024,512]{2,1,0:T(8,128)} fusion(f32[4,1024,512]{2,1,0:T(8,128)} %pad_maximum_fusion, s32[1024]{0:T(1024)S(1)} %pad_clamp_fusion), kind=kCustom, calls=%fused_computation.6 | custom fusion | bytes 16777232 | tf_op jit(solution)/shard_map/jit(_take)/gather | solution.py:205
  108.2 1.3 add.353
  109.5 2.7 %collective-permute-start.4 = (f32[256,512]{1,0:T(8,128)S(1)}, f32[256,512]{1,0:T(8,128)}, u32[]{:S(2)}, u32[]{:S(2)}) collective-permute-start(f32[256,512]{1,0:T(8,128)S(1)} %add.353), channel_id=1, source_target_pairs={{0,2},{1,3},{2,0},{3,1},{4,6},{5,7},{6,4},{7,5},{8,10},{9,11},{10,... | collective-permute-start | bytes 1572872 | tf_op jit(solution)/shard_map/ppermute | solution.py:141
  114.2 2.3 %gather_fusion.2 = f32[256]{0:T(256)S(1)} fusion(f32[256,256]{1,0:T(8,128)S(1)} %get-tuple-element.12, s32[256]{0:T(256)S(1)} %bitcast.88), kind=kCustom, calls=%fused_computation.2 | custom fusion | bytes 4096 | tf_op jit(solution)/shard_map/jit(_diag)/jit(diagonal)/cond/branch_0_fun/gather | solution.py:99
  116.6 2.3 %gather_fusion.4 = f32[256]{0:T(256)S(1)} fusion(f32[256,256]{1,0:T(8,128)S(1)} %get-tuple-element.13, s32[256]{0:T(256)S(1)} %bitcast.89), kind=kCustom, calls=%fused_computation.4 | custom fusion | bytes 4096 | tf_op jit(solution)/shard_map/jit(_diag)/jit(diagonal)/cond/branch_0_fun/gather | solution.py:99
  119.1 2.3 %gather_fusion.3 = f32[256]{0:T(256)S(1)} fusion(f32[256,256]{1,0:T(8,128)S(1)} %get-tuple-element.10, s32[256]{0:T(256)S(1)} %bitcast.90), kind=kCustom, calls=%fused_computation.3 | custom fusion | bytes 4096 | tf_op jit(solution)/shard_map/jit(_diag)/jit(diagonal)/cond/branch_0_fun/gather | solution.py:102
  128.6 7.3 %collective-permute-done.4 = f32[256,512]{1,0:T(8,128)} collective-permute-done((f32[256,512]{1,0:T(8,128)S(1)}, f32[256,512]{1,0:T(8,128)}, u32[]{:S(2)}, u32[]{:S(2)}) %collective-permute-start.4) | collective-permute-done | bytes 524320 | tf_op jit(solution)/shard_map/ppermute | solution.py:141
  138.2 2.6 %gather_fusion.5 = f32[256]{0:T(256)S(1)} fusion(f32[256,256]{1,0:T(8,128)S(1)} %get-tuple-element.11, s32[256]{0:T(256)S(1)} %bitcast.91), kind=kCustom, calls=%fused_computation.5 | custom fusion | bytes 4096 | tf_op jit(solution)/shard_map/jit(_diag)/jit(diagonal)/cond/branch_0_fun/gather | solution.py:102
  149.7 2.2 %bitcast_select_fusion = f32[4096,512]{1,0:T(8,128)S(1)} fusion(f32[4,1024,512]{2,1,0:T(8,128)S(1)} %bitcast.95, pred[4096]{0:T(1024)(128)(4,1)S(1)} %bitcast.98), kind=kLoop, calls=%fused_computation.8 | loop fusion | flops 2097152 | bytes 16781312 | tf_op jit(solution)/shard_map/jit(_take)/select_n | solution.py:205
  152.6 9.0 %convolution_subtract_fusion = f32[256,4096]{1,0:T(8,128)} fusion(f32[256,4096]{1,0:T(8,128)S(1)} %copy-done.2, f32[4096,512]{1,0:T(8,128)S(1)} %bitcast_select_fusion, f32[256,256]{0,1:T(8,128)S(1)} %fusion.25, f32[256,256]{0,1:T(8,128)S(1)} %fusion.26), kind=kOutput, calls=%fused_computation.9 | convolution fusion | flops 3222405120 | bytes 17301504 | tf_op jit(solution)/shard_map/rk,ck->rc/dot_general | solution.py:32
  161.7 7.5 %add_subtract_fusion = f32[128,4096]{1,0:T(8,128)} fusion(f32[128,4096]{1,0:T(8,128)} %collective-permute-done.11, f32[256,4096]{1,0:T(8,128)S(1)} %copy-done.4, f32[4096,512]{1,0:T(8,128)S(1)} %bitcast_select_fusion, f32[128,512]{1,0:T(8,128)S(1)} %collective-permute-done.13, f32[256,512]{1,0:T(8,128)S(1)} %slice_add_fusion.1), kind=kOutput, calls=%fused_computation.15 | convolution fusion | flops 1611726848 | bytes 15204352 | tf_op jit(solution)/shard_map/rk,ck->rc/dot_general | solution.py:32
  (119 shorter events, 29.3 us)
Async XLA Ops:
  9.9 4.8 %copy-start = (f32[512,4096]{1,0:T(8,128)}, f32[512,4096]{1,0:T(8,128)S(1)}, u32[]{:S(2)}) copy-start(f32[512,4096]{1,0:T(8,128)S(1)} %fusion.181) | copy-start | bytes 25165828
  9.9 5.3 %copy-start.6 = (f32[1024,256]{1,0:T(8,128)S(1)}, f32[1024,256]{1,0:T(8,128)}, u32[]{:S(2)}) copy-start(f32[1024,256]{1,0:T(8,128)} %param.7) | copy-start | bytes 3145732
  10.0 5.4 %copy-start.7 = (f32[1024,256]{1,0:T(8,128)S(1)}, f32[1024,256]{1,0:T(8,128)}, u32[]{:S(2)}) copy-start(f32[1024,256]{1,0:T(8,128)} %param.8) | copy-start | bytes 3145732
  14.7 59.2 %collective-permute-start.8 = (f32[256,4096]{1,0:T(8,128)}, f32[256,4096]{1,0:T(8,128)}, u32[]{:S(2)}, u32[]{:S(2)}) collective-permute-start(f32[256,4096]{1,0:T(8,128)} %slice.68), channel_id=1, source_target_pairs={{0,4},{4,0},{8,12},{12,8},{1,5},{5,1},{9,13},{13,9},{2,6},{6,2},{1... | collective-permute-start | bytes 12582920 | tf_op jit(solution)/shard_map/ppermute | solution.py:114
  15.6 54.8 %collective-permute-start = (f32[1024,512]{1,0:T(8,128)S(1)}, f32[1024,512]{1,0:T(8,128)}, u32[]{:S(2)}, u32[]{:S(2)}) collective-permute-start(f32[1024,512]{1,0:T(8,128)S(1)} %constant_dynamic-update-slice_fusion), channel_id=1, source_target_pairs={{0,4},{4,0},{8,12},{12,8},{1,5},{5,1},{9,13},{13,9},{2,6},{6,2},{1... | collective-permute-start | bytes 6291464 | tf_op jit(solution)/shard_map/ppermute | solution.py:114
  15.6 48.9 %collective-permute-start.1 = (f32[1,1024,512]{2,1,0:T(8,128)S(1)}, f32[1,1024,512]{2,1,0:T(8,128)}, u32[]{:S(2)}, u32[]{:S(2)}) collective-permute-start(f32[1,1024,512]{2,1,0:T(8,128)S(1)} %bitcast.92), channel_id=1, source_target_pairs={{0,8},{4,12},{8,0},{12,4},{1,9},{5,13},{9,1},{13,5},{2,10},{6,14},... | collective-permute-start | bytes 6291464 | tf_op jit(solution)/shard_map/ppermute | solution.py:114
  23.2 3.6 %collective-permute-start.5 = (f32[512,512]{1,0:T(8,128)}, f32[512,512]{1,0:T(8,128)}, u32[]{:S(2)}, u32[]{:S(2)}) collective-permute-start(f32[512,512]{1,0:T(8,128)} %fusion.180), channel_id=1, source_target_pairs={{0,4},{4,0},{8,12},{12,8},{1,5},{5,1},{9,13},{13,9},{2,6},{6,2},{1... | collective-permute-start | bytes 3145736 | tf_op jit(solution)/shard_map/ppermute | solution.py:114
  28.1 15.2 %collective-permute-start.6 = (f32[256,512]{1,0:T(8,128)S(1)}, f32[256,512]{1,0:T(8,128)S(1)}, u32[]{:S(2)}, u32[]{:S(2)}) collective-permute-start(f32[256,512]{1,0:T(8,128)S(1)} %dynamic-slice_add_fusion), channel_id=1, source_target_pairs={{0,1},{1,0},{2,3},{3,2},{4,5},{5,4},{6,7},{7,6},{8,9},{9,8},{10,11... | collective-permute-start | bytes 1572872 | tf_op jit(solution)/shard_map/ppermute | solution.py:141
  43.5 25.8 %collective-permute-start.7 = (f32[256,512]{1,0:T(8,128)S(1)}, f32[256,512]{1,0:T(8,128)}, u32[]{:S(2)}, u32[]{:S(2)}) collective-permute-start(f32[256,512]{1,0:T(8,128)S(1)} %add.359), channel_id=1, source_target_pairs={{0,2},{1,3},{2,0},{3,1},{4,6},{5,7},{6,4},{7,5},{8,10},{9,11},{10,... | collective-permute-start | bytes 1572872 | tf_op jit(solution)/shard_map/ppermute | solution.py:141
  46.4 24.0 %copy-start.1 = (f32[256,4096]{1,0:T(8,128)S(1)}, f32[256,4096]{1,0:T(8,128)}, u32[]{:S(2)}) copy-start(f32[256,4096]{1,0:T(8,128)} %param.6) | copy-start | bytes 12582916
  64.6 18.3 %collective-permute-start.2 = (f32[1,1024,512]{2,1,0:T(8,128)}, f32[1,1024,512]{2,1,0:T(8,128)S(1)}, u32[]{:S(2)}, u32[]{:S(2)}) collective-permute-start(f32[1,1024,512]{2,1,0:T(8,128)} %collective-permute-done.1), channel_id=1, source_target_pairs={{0,4},{4,0},{8,12},{12,8},{1,5},{5,1},{9,13},{13,9},{2,6},{6,2},{1... | collective-permute-start | bytes 6291464 | tf_op jit(solution)/shard_map/ppermute | solution.py:114
  77.9 13.9 %copy-start.3 = (f32[256,4096]{1,0:T(8,128)}, f32[256,4096]{1,0:T(8,128)S(1)}, u32[]{:S(2)}) copy-start(f32[256,4096]{1,0:T(8,128)S(1)} %slice_add_fusion) | copy-start | bytes 12582916
  77.9 13.0 %collective-permute-start.9 = (f32[256,512]{1,0:T(8,128)S(1)}, f32[256,512]{1,0:T(8,128)S(1)}, u32[]{:S(2)}, u32[]{:S(2)}) collective-permute-start(f32[256,512]{1,0:T(8,128)S(1)} %add.360), channel_id=1, source_target_pairs={{0,8},{4,12},{8,0},{12,4},{1,9},{5,13},{9,1},{13,5},{2,10},{6,14},... | collective-permute-start | bytes 1572872 | tf_op jit(solution)/shard_map/ppermute | solution.py:114
  85.1 15.4 %copy-start.5 = (f32[256,512]{1,0:T(8,128)}, f32[256,512]{1,0:T(8,128)S(1)}, u32[]{:S(2)}) copy-start(f32[256,512]{1,0:T(8,128)S(1)} %fusion.7) | copy-start | bytes 1572868
  85.1 23.1 %collective-permute-start.3 = (f32[256,512]{1,0:T(8,128)S(1)}, f32[256,512]{1,0:T(8,128)}, u32[]{:S(2)}, u32[]{:S(2)}) collective-permute-start(f32[256,512]{1,0:T(8,128)S(1)} %fusion.7), channel_id=1, source_target_pairs={{0,1},{1,0},{2,3},{3,2},{4,5},{5,4},{6,7},{7,6},{8,9},{9,8},{10,11... | collective-permute-start | bytes 1572872 | tf_op jit(solution)/shard_map/ppermute | solution.py:141
  91.8 20.3 %collective-permute-start.10 = (f32[256,512]{1,0:T(8,128)}, f32[256,512]{1,0:T(8,128)}, u32[]{:S(2)}, u32[]{:S(2)}) collective-permute-start(f32[256,512]{1,0:T(8,128)} %add.363), channel_id=1, source_target_pairs={{0,4},{4,0},{8,12},{12,8},{1,5},{5,1},{9,13},{13,9},{2,6},{6,2},{1... | collective-permute-start | bytes 1572872 | tf_op jit(solution)/shard_map/ppermute | solution.py:114
  93.3 68.3 %collective-permute-start.11 = (f32[128,4096]{1,0:T(8,128)}, f32[128,4096]{1,0:T(8,128)}, u32[]{:S(2)}, u32[]{:S(2)}) collective-permute-start(f32[128,4096]{1,0:T(8,128)} %slice.47), channel_id=1, source_target_pairs={{0,8},{4,12},{8,0},{12,4},{1,9},{5,13},{9,1},{13,5},{2,10},{6,14},... | collective-permute-start | bytes 6291464 | tf_op jit(solution)/shard_map/ppermute | solution.py:114
  109.5 26.4 %collective-permute-start.4 = (f32[256,512]{1,0:T(8,128)S(1)}, f32[256,512]{1,0:T(8,128)}, u32[]{:S(2)}, u32[]{:S(2)}) collective-permute-start(f32[256,512]{1,0:T(8,128)S(1)} %add.353), channel_id=1, source_target_pairs={{0,2},{1,3},{2,0},{3,1},{4,6},{5,7},{6,4},{7,5},{8,10},{9,11},{10,... | collective-permute-start | bytes 1572872 | tf_op jit(solution)/shard_map/ppermute | solution.py:141
  141.7 8.0 %slice-start = ((s8[8388608]{0:T(1024)(128)(4,1)}), s8[4194304]{0:T(1024)(128)(4,1)S(1)}, s32[]{:S(2)}) async-start(s8[8388608]{0:T(1024)(128)(4,1)} %bitcast.94), calls=%async_computation | async-start | bytes 8388608
  145.7 4.0 %slice-start.1 = ((s8[8388608]{0:T(1024)(128)(4,1)}), s8[4194304]{0:T(1024)(128)(4,1)S(1)}, s32[]{:S(2)}) async-start(s8[8388608]{0:T(1024)(128)(4,1)} %bitcast.94), calls=%async_computation.1 | async-start | bytes 8388608
  149.6 2.3 %collective-permute-start.12 = (f32[256,512]{1,0:T(8,128)S(1)}, f32[256,512]{1,0:T(8,128)S(1)}, u32[]{:S(2)}, u32[]{:S(2)}) collective-permute-start(f32[256,512]{1,0:T(8,128)S(1)} %slice.74), channel_id=1, source_target_pairs={{0,4},{4,0},{8,12},{12,8},{1,5},{5,1},{9,13},{13,9},{2,6},{6,2},{1... | collective-permute-start | bytes 1572872 | tf_op jit(solution)/shard_map/ppermute | solution.py:114
  149.7 2.9 %copy-start.2 = (f32[256,4096]{1,0:T(8,128)S(1)}, f32[256,4096]{1,0:T(8,128)}, u32[]{:S(2)}) copy-start(f32[256,4096]{1,0:T(8,128)} %param.6) | copy-start | bytes 12582916
  152.1 9.6 %copy-start.4 = (f32[256,4096]{1,0:T(8,128)S(1)}, f32[256,4096]{1,0:T(8,128)}, u32[]{:S(2)}) copy-start(f32[256,4096]{1,0:T(8,128)} %copy-done.3) | copy-start | bytes 12582916
  152.1 9.6 %collective-permute-start.13 = (f32[128,512]{1,0:T(8,128)S(1)}, f32[128,512]{1,0:T(8,128)S(1)}, u32[]{:S(2)}, u32[]{:S(2)}) collective-permute-start(f32[128,512]{1,0:T(8,128)S(1)} %slice.76), channel_id=1, source_target_pairs={{0,8},{4,12},{8,0},{12,4},{1,9},{5,13},{9,1},{13,5},{2,10},{6,14},... | collective-permute-start | bytes 786440 | tf_op jit(solution)/shard_map/ppermute | solution.py:114
where the time goes:
time: 172 us; the launch traced here: 169 us
  matrix products  56.4 us (33%)
  waiting for transfers between devices  47.8 us (28%)
  local copies, waits for them, and re-layouts  27.1 us (16%)
  other arithmetic  20 us (12%)
  starting transfers between devices  16.4 us (10%)
    dot_general x39, matrix products, dot_high(): jnp.dot(left, right, precision=lax.Precision.HIGHEST, preferred_element_t...  28.1 us
    ppermute x10, waiting for transfers between devices, swap(): return lax.ppermute(value, 'row', [(i, i ^ distance) for i in range(size)])  26.9 us
    ppermute x4, waiting for transfers between devices, col_sum(): lax.ppermute(value, 'col', [(i, i ^ distance) for i in range(size)])  20.9 us
    dot_general x2, matrix products, outer_mid(): jnp.einsum('rk,ck->rc', left, right, precision=lax.Precision.HIGH, prefer...  16.5 us
    ppermute x4, starting transfers between devices, col_sum(): lax.ppermute(value, 'col', [(i, i ^ distance) for i in range(size)])  9.1 us
    gather x1, local copies, waits for them, and re-layouts, shards(): jnp.take(held, jnp.arange(size) ^ me, axis=0).reshape(size * span, -1)  7.74 us
    ppermute x10, starting transfers between devices, swap(): return lax.ppermute(value, 'row', [(i, i ^ distance) for i in range(size)])  7.26 us
    dot_general x1, matrix products, inner_mid(): jnp.einsum('ra,rb->ab', left, right, precision=lax.Precision.HIGH, prefer...  6.16 us
  transfers between devices with their start and end apart: 14, of which 6 were waited for; matrix products, arithmetic and copies ran while one was open for 48% of the time, Pallas kernels for 0%

commit v1 on v0

--- a/solution.py
+++ b/solution.py
@@ -198,7 +198,7 @@
     image = None
     for slot in range(size):
         cols = lax.dynamic_slice_in_dim(basis, (me ^ slot) * span, span, axis=1)
-        part = dot_high(cols, held[slot])
+        part = jnp.dot(cols, held[slot], precision=lax.Precision.HIGH, preferred_element_type=jnp.float32)
         image = part if image is None else image + part
     image = col_sum(image)
 

time: 172 us -> 171 us (level)
  matrix products: 56.4 us -> 53.1 us
  waiting for transfers between devices: 47.8 us -> 50.5 us
    dot_general x39 -> x35, matrix products: 28.1 us -> 15.8 us  [dot_high(): jnp.dot(left, right, precision=lax.Precision.HIGHEST, preferred_element_t...]
    dot_general x0 -> x4, matrix products: none -> 9.01 us  [shards(): jnp.dot(cols, held[slot], precision=lax.Precision.HIGH, preferred_element...]
    ppermute x10, waiting for transfers between devices: 26.9 us -> 28.7 us  [swap(): return lax.ppermute(value, 'row', [(i, i ^ distance) for i in range(size)])]
  transfers between devices with their start and end apart: 14 -> 14, of which waited for: 6 -> 6; matrix products, arithmetic and copies ran while one was open for 48% -> 47% of each run, Pallas kernels for 0% -> 0%
where the time goes in v1:
time: 171 us; the launch traced here: 168 us
  matrix products  53.1 us (31%)
  waiting for transfers between devices  50.5 us (30%)
  local copies, waits for them, and re-layouts  27.3 us (16%)
  other arithmetic  20 us (12%)
  starting transfers between devices  15.9 us (9%)
    ppermute x10, waiting for transfers between devices, swap(): return lax.ppermute(value, 'row', [(i, i ^ distance) for i in range(size)])  28.7 us
    ppermute x4, waiting for transfers between devices, col_sum(): lax.ppermute(value, 'col', [(i, i ^ distance) for i in range(size)])  21.8 us
    dot_general x2, matrix products, outer_mid(): jnp.einsum('rk,ck->rc', left, right, precision=lax.Precision.HIGH, prefer...  16.5 us
    dot_general x35, matrix products, dot_high(): jnp.dot(left, right, precision=lax.Precision.HIGHEST, preferred_element_t...  15.8 us
    dot_general x4, matrix products, shards(): jnp.dot(cols, held[slot], precision=lax.Precision.HIGH, preferred_element...  9.01 us
    ppermute x4, starting transfers between devices, col_sum(): lax.ppermute(value, 'col', [(i, i ^ distance) for i in range(size)])  8.76 us
    gather x1, local copies, waits for them, and re-layouts, shards(): jnp.take(held, jnp.arange(size) ^ me, axis=0).reshape(size * span, -1)  7.74 us
    ppermute x10, starting transfers between devices, swap(): return lax.ppermute(value, 'row', [(i, i ^ distance) for i in range(size)])  7.16 us
  transfers between devices with their start and end apart: 14, of which 6 were waited for; matrix products, arithmetic and copies ran while one was open for 47% of the time, Pallas kernels for 0%

profile of v1, /device:TPU:0, one launch (start us, length us, event | category | flops | bytes accessed | tf_op | source)
XLA Modules:
  0.0 168.4 jit_solution(9327457964316006121)
XLA Ops:
  3.8 6.2 %fusion.181 = f32[512,4096]{1,0:T(8,128)S(1)} fusion(f32[256,512]{0,1:T(8,128)S(1)} %bitcast_select_fusion.2, f32[256,4096]{1,0:T(8,128)} %param.6), kind=kOutput, calls=%fused_computation.307 | convolution fusion | flops 3221225472 | bytes 13107200 | tf_op jit(solution)/shard_map/ra,rb->ab/dot_general | solution.py:42
  10.0 2.5 %slice.68 = f32[256,4096]{1,0:T(8,128)} slice(f32[512,4096]{1,0:T(8,128)S(1)} %fusion.181), slice={[0:256], [0:4096]} | slice | bytes 8388608 | tf_op jit(solution)/shard_map/slice | solution.py:180
  12.4 2.3 %copy-done = f32[512,4096]{1,0:T(8,128)} copy-done((f32[512,4096]{1,0:T(8,128)}, f32[512,4096]{1,0:T(8,128)S(1)}, u32[]{:S(2)}) %copy-start) | copy-done | bytes 8388632
  15.6 3.0 %collective-permute-start.1 = (f32[1,1024,512]{2,1,0:T(8,128)S(1)}, f32[1,1024,512]{2,1,0:T(8,128)}, u32[]{:S(2)}, u32[]{:S(2)}) collective-permute-start(f32[1,1024,512]{2,1,0:T(8,128)S(1)} %bitcast.92), channel_id=1, source_target_pairs={{0,8},{4,12},{8,0},{12,4},{1,9},{5,13},{9,1},{13,5},{2,10},{6,14},... | collective-permute-start | bytes 6291464 | tf_op jit(solution)/shard_map/ppermute | solution.py:114
  18.6 4.6 %fusion.180 = f32[512,512]{1,0:T(8,128)} fusion(f32[1024,512]{1,0:T(8,128)S(1)} %constant_dynamic-update-slice_fusion), kind=kOutput, calls=%fused_computation.306 | convolution fusion | flops 3221225472 | bytes 3145728 | tf_op jit(solution)/shard_map/ra,rb->ab/dot_general | solution.py:12
  23.4 3.5 %collective-permute-done.5 = f32[512,512]{1,0:T(8,128)} collective-permute-done((f32[512,512]{1,0:T(8,128)}, f32[512,512]{1,0:T(8,128)}, u32[]{:S(2)}, u32[]{:S(2)}) %collective-permute-start.5) | collective-permute-done | bytes 1048608 | tf_op jit(solution)/shard_map/ppermute | solution.py:114
  26.9 1.3 dynamic-slice_add_fusion
  28.1 3.0 %collective-permute-start.6 = (f32[256,512]{1,0:T(8,128)S(1)}, f32[256,512]{1,0:T(8,128)S(1)}, u32[]{:S(2)}, u32[]{:S(2)}) collective-permute-start(f32[256,512]{1,0:T(8,128)S(1)} %dynamic-slice_add_fusion), channel_id=1, source_target_pairs={{0,1},{1,0},{2,3},{3,2},{4,5},{5,4},{6,7},{7,6},{8,9},{9,8},{10,11... | collective-permute-start | bytes 1572872 | tf_op jit(solution)/shard_map/ppermute | solution.py:141
  31.2 12.1 %collective-permute-done.6 = f32[256,512]{1,0:T(8,128)S(1)} collective-permute-done((f32[256,512]{1,0:T(8,128)S(1)}, f32[256,512]{1,0:T(8,128)S(1)}, u32[]{:S(2)}, u32[]{:S(2)}) %collective-permute-start.6) | collective-permute-done | bytes 524320 | tf_op jit(solution)/shard_map/ppermute | solution.py:141
  43.5 2.8 %collective-permute-start.7 = (f32[256,512]{1,0:T(8,128)S(1)}, f32[256,512]{1,0:T(8,128)}, u32[]{:S(2)}, u32[]{:S(2)}) collective-permute-start(f32[256,512]{1,0:T(8,128)S(1)} %add.359), channel_id=1, source_target_pairs={{0,2},{1,3},{2,0},{3,1},{4,6},{5,7},{6,4},{7,5},{8,10},{9,11},{10,... | collective-permute-start | bytes 1572872 | tf_op jit(solution)/shard_map/ppermute | solution.py:141
  46.4 18.2 %collective-permute-done.1 = f32[1,1024,512]{2,1,0:T(8,128)} collective-permute-done((f32[1,1024,512]{2,1,0:T(8,128)S(1)}, f32[1,1024,512]{2,1,0:T(8,128)}, u32[]{:S(2)}, u32[]{:S(2)}) %collective-permute-start.1) | collective-permute-done | bytes 2097184 | tf_op jit(solution)/shard_map/ppermute | solution.py:114
  64.6 2.4 %fusion.13 = f32[256,512]{1,0:T(8,128)S(1)} fusion(f32[1024,512]{1,0:T(8,128)S(1)} %constant_dynamic-update-slice_fusion, f32[256,4096]{1,0:T(8,128)} %param.6, s32[]{:T(128)S(6)} %select_n.477), kind=kOutput, calls=%fused_computation.40 | convolution fusion | flops 805306368 | bytes 3670020 | tf_op jit(solution)/shard_map/dot_general | solution.py:201
  67.0 2.2 %collective-permute-done.7 = f32[256,512]{1,0:T(8,128)} collective-permute-done((f32[256,512]{1,0:T(8,128)S(1)}, f32[256,512]{1,0:T(8,128)}, u32[]{:S(2)}, u32[]{:S(2)}) %collective-permute-start.7) | collective-permute-done | bytes 524320 | tf_op jit(solution)/shard_map/ppermute | solution.py:141
  70.4 2.7 %convolution_add_fusion = f32[256,512]{1,0:T(8,128)S(1)} fusion(f32[256,512]{1,0:T(8,128)S(1)} %fusion.13, f32[1024,512]{1,0:T(8,128)} %collective-permute-done, f32[256,4096]{1,0:T(8,128)S(1)} %copy-done.1, s32[]{:T(128)S(6)} %select_n.478), kind=kOutput, calls=%fused_computation.18 | convolution fusion | flops 805437440 | bytes 4194308 | tf_op jit(solution)/shard_map/dot_general | solution.py:201
  73.1 3.9 %slice_add_fusion = f32[256,4096]{1,0:T(8,128)S(1)} fusion(f32[256,4096]{1,0:T(8,128)} %collective-permute-done.8, f32[512,4096]{1,0:T(8,128)} %copy-done), kind=kLoop, calls=%fused_computation.10 | loop fusion | flops 1048576 | bytes 12582912 | tf_op jit(solution)/shard_map/add | solution.py:180
  77.1 1.4 collective-permute-start.9
  78.5 2.7 %fusion.4 = f32[256,512]{1,0:T(8,128)S(1)} fusion(f32[256,512]{1,0:T(8,128)S(1)} %convolution_add_fusion, f32[1,1024,512]{2,1,0:T(8,128)} %collective-permute-done.1, f32[256,4096]{1,0:T(8,128)S(1)} %copy-done.1, s32[]{:T(128)S(6)} %select_n.479), kind=kOutput, calls=%fused_computation.16 | convolution fusion | flops 805437440 | bytes 4194308 | tf_op jit(solution)/shard_map/dot_general | solution.py:201
  83.1 7.0 %collective-permute-done.9 = f32[256,512]{1,0:T(8,128)S(1)} collective-permute-done((f32[256,512]{1,0:T(8,128)S(1)}, f32[256,512]{1,0:T(8,128)S(1)}, u32[]{:S(2)}, u32[]{:S(2)}) %collective-permute-start.9) | collective-permute-done | bytes 524320 | tf_op jit(solution)/shard_map/ppermute | solution.py:114
  91.0 1.5 slice.47
  93.7 5.5 %pad_maximum_fusion = f32[4,1024,512]{2,1,0:T(8,128)} fusion(f32[1,1024,512]{2,1,0:T(8,128)S(1)} %collective-permute-done.2, f32[1,1024,512]{2,1,0:T(8,128)} %collective-permute-done.1, f32[1,1024,512]{2,1,0:T(8,128)} %bitcast.11, f32[1,1024,512]{2,1,0:T(8,128)S(1)} %bitcast.93), kind=kLoop, calls=%fused_computation.7 | loop fusion | flops 6291456 | bytes 16777216 | tf_op jit(solution)/shard_map/stack | solution.py:174
  99.2 7.7 %gather_fusion.6 = f32[4,1024,512]{2,1,0:T(8,128)} fusion(f32[4,1024,512]{2,1,0:T(8,128)} %pad_maximum_fusion, s32[1024]{0:T(1024)S(1)} %pad_clamp_fusion), kind=kCustom, calls=%fused_computation.6 | custom fusion | bytes 16777232 | tf_op jit(solution)/shard_map/jit(_take)/gather | solution.py:205
  107.0 1.3 add.353
  108.2 2.3 %collective-permute-start.4 = (f32[256,512]{1,0:T(8,128)S(1)}, f32[256,512]{1,0:T(8,128)}, u32[]{:S(2)}, u32[]{:S(2)}) collective-permute-start(f32[256,512]{1,0:T(8,128)S(1)} %add.353), channel_id=1, source_target_pairs={{0,2},{1,3},{2,0},{3,1},{4,6},{5,7},{6,4},{7,5},{8,10},{9,11},{10,... | collective-permute-start | bytes 1572872 | tf_op jit(solution)/shard_map/ppermute | solution.py:141
  110.6 1.3 pad_maximum_fusion.1
  112.6 2.5 %gather_fusion.2 = f32[256]{0:T(256)S(1)} fusion(f32[256,256]{1,0:T(8,128)S(1)} %get-tuple-element.12, s32[256]{0:T(256)S(1)} %bitcast.88), kind=kCustom, calls=%fused_computation.2 | custom fusion | bytes 4096 | tf_op jit(solution)/shard_map/jit(_diag)/jit(diagonal)/cond/branch_0_fun/gather | solution.py:99
  115.2 2.3 %gather_fusion.4 = f32[256]{0:T(256)S(1)} fusion(f32[256,256]{1,0:T(8,128)S(1)} %get-tuple-element.13, s32[256]{0:T(256)S(1)} %bitcast.89), kind=kCustom, calls=%fused_computation.4 | custom fusion | bytes 4096 | tf_op jit(solution)/shard_map/jit(_diag)/jit(diagonal)/cond/branch_0_fun/gather | solution.py:99
  117.7 2.3 %gather_fusion.3 = f32[256]{0:T(256)S(1)} fusion(f32[256,256]{1,0:T(8,128)S(1)} %get-tuple-element.10, s32[256]{0:T(256)S(1)} %bitcast.90), kind=kCustom, calls=%fused_computation.3 | custom fusion | bytes 4096 | tf_op jit(solution)/shard_map/jit(_diag)/jit(diagonal)/cond/branch_0_fun/gather | solution.py:102
  127.1 7.5 %collective-permute-done.4 = f32[256,512]{1,0:T(8,128)} collective-permute-done((f32[256,512]{1,0:T(8,128)S(1)}, f32[256,512]{1,0:T(8,128)}, u32[]{:S(2)}, u32[]{:S(2)}) %collective-permute-start.4) | collective-permute-done | bytes 524320 | tf_op jit(solution)/shard_map/ppermute | solution.py:141
  137.0 2.6 %gather_fusion.5 = f32[256]{0:T(256)S(1)} fusion(f32[256,256]{1,0:T(8,128)S(1)} %get-tuple-element.11, s32[256]{0:T(256)S(1)} %bitcast.91), kind=kCustom, calls=%fused_computation.5 | custom fusion | bytes 4096 | tf_op jit(solution)/shard_map/jit(_diag)/jit(diagonal)/cond/branch_0_fun/gather | solution.py:102
  148.5 2.2 %bitcast_select_fusion = f32[4096,512]{1,0:T(8,128)S(1)} fusion(f32[4,1024,512]{2,1,0:T(8,128)S(1)} %bitcast.95, pred[4096]{0:T(1024)(128)(4,1)S(1)} %bitcast.98), kind=kLoop, calls=%fused_computation.8 | loop fusion | flops 2097152 | bytes 16781312 | tf_op jit(solution)/shard_map/jit(_take)/select_n | solution.py:205
  151.7 9.0 %convolution_subtract_fusion = f32[256,4096]{1,0:T(8,128)} fusion(f32[256,4096]{1,0:T(8,128)S(1)} %copy-done.2, f32[4096,512]{1,0:T(8,128)S(1)} %bitcast_select_fusion, f32[256,256]{0,1:T(8,128)S(1)} %fusion.25, f32[256,256]{0,1:T(8,128)S(1)} %fusion.26), kind=kOutput, calls=%fused_computation.9 | convolution fusion | flops 3222405120 | bytes 17301504 | tf_op jit(solution)/shard_map/rk,ck->rc/dot_general | solution.py:32
  160.7 7.5 %add_subtract_fusion = f32[128,4096]{1,0:T(8,128)} fusion(f32[128,4096]{1,0:T(8,128)} %collective-permute-done.11, f32[256,4096]{1,0:T(8,128)S(1)} %copy-done.4, f32[4096,512]{1,0:T(8,128)S(1)} %bitcast_select_fusion, f32[128,512]{1,0:T(8,128)S(1)} %collective-permute-done.13, f32[256,512]{1,0:T(8,128)S(1)} %slice_add_fusion.1), kind=kOutput, calls=%fused_computation.15 | convolution fusion | flops 1611726848 | bytes 15204352 | tf_op jit(solution)/shard_map/rk,ck->rc/dot_general | solution.py:32
  (119 shorter events, 29.5 us)
Async XLA Ops:
  9.9 4.8 %copy-start = (f32[512,4096]{1,0:T(8,128)}, f32[512,4096]{1,0:T(8,128)S(1)}, u32[]{:S(2)}) copy-start(f32[512,4096]{1,0:T(8,128)S(1)} %fusion.181) | copy-start | bytes 25165828
  9.9 5.3 %copy-start.6 = (f32[1024,256]{1,0:T(8,128)S(1)}, f32[1024,256]{1,0:T(8,128)}, u32[]{:S(2)}) copy-start(f32[1024,256]{1,0:T(8,128)} %param.7) | copy-start | bytes 3145732
  10.0 5.4 %copy-start.7 = (f32[1024,256]{1,0:T(8,128)S(1)}, f32[1024,256]{1,0:T(8,128)}, u32[]{:S(2)}) copy-start(f32[1024,256]{1,0:T(8,128)} %param.8) | copy-start | bytes 3145732
  14.7 58.4 %collective-permute-start.8 = (f32[256,4096]{1,0:T(8,128)}, f32[256,4096]{1,0:T(8,128)}, u32[]{:S(2)}, u32[]{:S(2)}) collective-permute-start(f32[256,4096]{1,0:T(8,128)} %slice.68), channel_id=1, source_target_pairs={{0,4},{4,0},{8,12},{12,8},{1,5},{5,1},{9,13},{13,9},{2,6},{6,2},{1... | collective-permute-start | bytes 12582920 | tf_op jit(solution)/shard_map/ppermute | solution.py:114
  15.6 54.8 %collective-permute-start = (f32[1024,512]{1,0:T(8,128)S(1)}, f32[1024,512]{1,0:T(8,128)}, u32[]{:S(2)}, u32[]{:S(2)}) collective-permute-start(f32[1024,512]{1,0:T(8,128)S(1)} %constant_dynamic-update-slice_fusion), channel_id=1, source_target_pairs={{0,4},{4,0},{8,12},{12,8},{1,5},{5,1},{9,13},{13,9},{2,6},{6,2},{1... | collective-permute-start | bytes 6291464 | tf_op jit(solution)/shard_map/ppermute | solution.py:114
  15.6 48.9 %collective-permute-start.1 = (f32[1,1024,512]{2,1,0:T(8,128)S(1)}, f32[1,1024,512]{2,1,0:T(8,128)}, u32[]{:S(2)}, u32[]{:S(2)}) collective-permute-start(f32[1,1024,512]{2,1,0:T(8,128)S(1)} %bitcast.92), channel_id=1, source_target_pairs={{0,8},{4,12},{8,0},{12,4},{1,9},{5,13},{9,1},{13,5},{2,10},{6,14},... | collective-permute-start | bytes 6291464 | tf_op jit(solution)/shard_map/ppermute | solution.py:114
  23.2 3.6 %collective-permute-start.5 = (f32[512,512]{1,0:T(8,128)}, f32[512,512]{1,0:T(8,128)}, u32[]{:S(2)}, u32[]{:S(2)}) collective-permute-start(f32[512,512]{1,0:T(8,128)} %fusion.180), channel_id=1, source_target_pairs={{0,4},{4,0},{8,12},{12,8},{1,5},{5,1},{9,13},{13,9},{2,6},{6,2},{1... | collective-permute-start | bytes 3145736 | tf_op jit(solution)/shard_map/ppermute | solution.py:114
  28.1 15.2 %collective-permute-start.6 = (f32[256,512]{1,0:T(8,128)S(1)}, f32[256,512]{1,0:T(8,128)S(1)}, u32[]{:S(2)}, u32[]{:S(2)}) collective-permute-start(f32[256,512]{1,0:T(8,128)S(1)} %dynamic-slice_add_fusion), channel_id=1, source_target_pairs={{0,1},{1,0},{2,3},{3,2},{4,5},{5,4},{6,7},{7,6},{8,9},{9,8},{10,11... | collective-permute-start | bytes 1572872 | tf_op jit(solution)/shard_map/ppermute | solution.py:141
  43.5 25.8 %collective-permute-start.7 = (f32[256,512]{1,0:T(8,128)S(1)}, f32[256,512]{1,0:T(8,128)}, u32[]{:S(2)}, u32[]{:S(2)}) collective-permute-start(f32[256,512]{1,0:T(8,128)S(1)} %add.359), channel_id=1, source_target_pairs={{0,2},{1,3},{2,0},{3,1},{4,6},{5,7},{6,4},{7,5},{8,10},{9,11},{10,... | collective-permute-start | bytes 1572872 | tf_op jit(solution)/shard_map/ppermute | solution.py:141
  46.4 24.0 %copy-start.1 = (f32[256,4096]{1,0:T(8,128)S(1)}, f32[256,4096]{1,0:T(8,128)}, u32[]{:S(2)}) copy-start(f32[256,4096]{1,0:T(8,128)} %param.6) | copy-start | bytes 12582916
  64.6 16.6 %collective-permute-start.2 = (f32[1,1024,512]{2,1,0:T(8,128)}, f32[1,1024,512]{2,1,0:T(8,128)S(1)}, u32[]{:S(2)}, u32[]{:S(2)}) collective-permute-start(f32[1,1024,512]{2,1,0:T(8,128)} %collective-permute-done.1), channel_id=1, source_target_pairs={{0,4},{4,0},{8,12},{12,8},{1,5},{5,1},{9,13},{13,9},{2,6},{6,2},{1... | collective-permute-start | bytes 6291464 | tf_op jit(solution)/shard_map/ppermute | solution.py:114
  77.1 13.9 %copy-start.3 = (f32[256,4096]{1,0:T(8,128)}, f32[256,4096]{1,0:T(8,128)S(1)}, u32[]{:S(2)}) copy-start(f32[256,4096]{1,0:T(8,128)S(1)} %slice_add_fusion) | copy-start | bytes 12582916
  77.1 13.0 %collective-permute-start.9 = (f32[256,512]{1,0:T(8,128)S(1)}, f32[256,512]{1,0:T(8,128)S(1)}, u32[]{:S(2)}, u32[]{:S(2)}) collective-permute-start(f32[256,512]{1,0:T(8,128)S(1)} %add.360), channel_id=1, source_target_pairs={{0,8},{4,12},{8,0},{12,4},{1,9},{5,13},{9,1},{13,5},{2,10},{6,14},... | collective-permute-start | bytes 1572872 | tf_op jit(solution)/shard_map/ppermute | solution.py:114
  82.5 16.8 %copy-start.5 = (f32[256,512]{1,0:T(8,128)}, f32[256,512]{1,0:T(8,128)S(1)}, u32[]{:S(2)}) copy-start(f32[256,512]{1,0:T(8,128)S(1)} %fusion.7) | copy-start | bytes 1572868
  82.5 24.5 %collective-permute-start.3 = (f32[256,512]{1,0:T(8,128)S(1)}, f32[256,512]{1,0:T(8,128)}, u32[]{:S(2)}, u32[]{:S(2)}) collective-permute-start(f32[256,512]{1,0:T(8,128)S(1)} %fusion.7), channel_id=1, source_target_pairs={{0,1},{1,0},{2,3},{3,2},{4,5},{5,4},{6,7},{7,6},{8,9},{9,8},{10,11... | collective-permute-start | bytes 1572872 | tf_op jit(solution)/shard_map/ppermute | solution.py:141
  91.0 19.6 %collective-permute-start.10 = (f32[256,512]{1,0:T(8,128)}, f32[256,512]{1,0:T(8,128)}, u32[]{:S(2)}, u32[]{:S(2)}) collective-permute-start(f32[256,512]{1,0:T(8,128)} %add.363), channel_id=1, source_target_pairs={{0,4},{4,0},{8,12},{12,8},{1,5},{5,1},{9,13},{13,9},{2,6},{6,2},{1... | collective-permute-start | bytes 1572872 | tf_op jit(solution)/shard_map/ppermute | solution.py:114
  92.5 68.2 %collective-permute-start.11 = (f32[128,4096]{1,0:T(8,128)}, f32[128,4096]{1,0:T(8,128)}, u32[]{:S(2)}, u32[]{:S(2)}) collective-permute-start(f32[128,4096]{1,0:T(8,128)} %slice.47), channel_id=1, source_target_pairs={{0,8},{4,12},{8,0},{12,4},{1,9},{5,13},{9,1},{13,5},{2,10},{6,14},... | collective-permute-start | bytes 6291464 | tf_op jit(solution)/shard_map/ppermute | solution.py:114
  108.2 26.4 %collective-permute-start.4 = (f32[256,512]{1,0:T(8,128)S(1)}, f32[256,512]{1,0:T(8,128)}, u32[]{:S(2)}, u32[]{:S(2)}) collective-permute-start(f32[256,512]{1,0:T(8,128)S(1)} %add.353), channel_id=1, source_target_pairs={{0,2},{1,3},{2,0},{3,1},{4,6},{5,7},{6,4},{7,5},{8,10},{9,11},{10,... | collective-permute-start | bytes 1572872 | tf_op jit(solution)/shard_map/ppermute | solution.py:141
  140.4 8.0 %slice-start = ((s8[8388608]{0:T(1024)(128)(4,1)}), s8[4194304]{0:T(1024)(128)(4,1)S(1)}, s32[]{:S(2)}) async-start(s8[8388608]{0:T(1024)(128)(4,1)} %bitcast.94), calls=%async_computation | async-start | bytes 8388608
  144.5 4.0 %slice-start.1 = ((s8[8388608]{0:T(1024)(128)(4,1)}), s8[4194304]{0:T(1024)(128)(4,1)S(1)}, s32[]{:S(2)}) async-start(s8[8388608]{0:T(1024)(128)(4,1)} %bitcast.94), calls=%async_computation.1 | async-start | bytes 8388608
  148.4 2.3 %collective-permute-start.12 = (f32[256,512]{1,0:T(8,128)S(1)}, f32[256,512]{1,0:T(8,128)S(1)}, u32[]{:S(2)}, u32[]{:S(2)}) collective-permute-start(f32[256,512]{1,0:T(8,128)S(1)} %slice.74), channel_id=1, source_target_pairs={{0,4},{4,0},{8,12},{12,8},{1,5},{5,1},{9,13},{13,9},{2,6},{6,2},{1... | collective-permute-start | bytes 1572872 | tf_op jit(solution)/shard_map/ppermute | solution.py:114
  148.5 3.2 %copy-start.2 = (f32[256,4096]{1,0:T(8,128)S(1)}, f32[256,4096]{1,0:T(8,128)}, u32[]{:S(2)}) copy-start(f32[256,4096]{1,0:T(8,128)} %param.6) | copy-start | bytes 12582916
  150.8 9.9 %copy-start.4 = (f32[256,4096]{1,0:T(8,128)S(1)}, f32[256,4096]{1,0:T(8,128)}, u32[]{:S(2)}) copy-start(f32[256,4096]{1,0:T(8,128)} %copy-done.3) | copy-start | bytes 12582916
  150.8 9.9 %collective-permute-start.13 = (f32[128,512]{1,0:T(8,128)S(1)}, f32[128,512]{1,0:T(8,128)S(1)}, u32[]{:S(2)}, u32[]{:S(2)}) collective-permute-start(f32[128,512]{1,0:T(8,128)S(1)} %slice.76), channel_id=1, source_target_pairs={{0,8},{4,12},{8,0},{12,4},{1,9},{5,13},{9,1},{13,5},{2,10},{6,14},... | collective-permute-start | bytes 786440 | tf_op jit(solution)/shard_map/ppermute | solution.py:114

commit v2 on v0

--- a/solution.py
+++ b/solution.py
@@ -200,7 +200,7 @@
         cols = lax.dynamic_slice_in_dim(basis, (me ^ slot) * span, span, axis=1)
         part = dot_high(cols, held[slot])
         image = part if image is None else image + part
-    image = col_sum(image)
+    image = jnp.concatenate([col_sum(image[:, :k]), col_sum(image[:, k:])], axis=1)
 
     gathered = jnp.take(held, jnp.arange(size) ^ me, axis=0).reshape(size * span, -1)
     factor_one = tri_factor_doubling(gram[:k, :k])

time: 172 us -> 170 us (0.988)
  waiting for transfers between devices: 47.8 us -> 41.6 us
    ppermute x4 -> x6, waiting for transfers between devices: 20.9 us -> 13.6 us  [col_sum(): lax.ppermute(value, 'col', [(i, i ^ distance) for i in range(size)])]
    ppermute x4 -> x6, starting transfers between devices: 9.1 us -> 10.8 us  [col_sum(): lax.ppermute(value, 'col', [(i, i ^ distance) for i in range(size)])]
    add x4 -> x3, other arithmetic: 3.66 us -> 3.07 us  [col_sum(): value + lax.ppermute(value, 'col', [(i, i ^ distance) for i in range(size)])]
  transfers between devices with their start and end apart: 14 -> 16, of which waited for: 6 -> 5; matrix products, arithmetic and copies ran while one was open for 48% -> 50% of each run, Pallas kernels for 0% -> 0%
where the time goes in v2:
time: 170 us; the launch traced here: 167 us
  matrix products  57.8 us (34%)
  waiting for transfers between devices  41.6 us (24%)
  local copies, waits for them, and re-layouts  28.6 us (17%)
  other arithmetic  19.4 us (11%)
  starting transfers between devices  17.9 us (11%)
  between operations  1.7 us (1%)
    dot_general x39, matrix products, dot_high(): jnp.dot(left, right, precision=lax.Precision.HIGHEST, preferred_element_t...  29.5 us
    ppermute x10, waiting for transfers between devices, swap(): return lax.ppermute(value, 'row', [(i, i ^ distance) for i in range(size)])  27.9 us
    dot_general x2, matrix products, outer_mid(): jnp.einsum('rk,ck->rc', left, right, precision=lax.Precision.HIGH, prefer...  16.5 us
    ppermute x6, waiting for transfers between devices, col_sum(): lax.ppermute(value, 'col', [(i, i ^ distance) for i in range(size)])  13.6 us
    ppermute x6, starting transfers between devices, col_sum(): lax.ppermute(value, 'col', [(i, i ^ distance) for i in range(size)])  10.8 us
    gather x1, local copies, waits for them, and re-layouts, shards(): jnp.take(held, jnp.arange(size) ^ me, axis=0).reshape(size * span, -1)  7.74 us
    ppermute x10, starting transfers between devices, swap(): return lax.ppermute(value, 'row', [(i, i ^ distance) for i in range(size)])  7.17 us
    dot_general x1, matrix products, inner_mid(): jnp.einsum('ra,rb->ab', left, right, precision=lax.Precision.HIGH, prefer...  6.16 us
  transfers between devices with their start and end apart: 16, of which 5 were waited for; matrix products, arithmetic and copies ran while one was open for 50% of the time, Pallas kernels for 0%

profile of v2, /device:TPU:0, one launch (start us, length us, event | category | flops | bytes accessed | tf_op | source)
XLA Modules:
  0.0 167.0 jit_solution(17367065743423190643)
XLA Ops:
  3.8 6.2 %fusion.184 = f32[512,4096]{1,0:T(8,128)S(1)} fusion(f32[256,512]{0,1:T(8,128)S(1)} %bitcast_select_fusion.2, f32[256,4096]{1,0:T(8,128)} %param.6), kind=kOutput, calls=%fused_computation.311 | convolution fusion | flops 3221225472 | bytes 13107200 | tf_op jit(solution)/shard_map/ra,rb->ab/dot_general | solution.py:42
  10.0 2.5 %slice.68 = f32[256,4096]{1,0:T(8,128)} slice(f32[512,4096]{1,0:T(8,128)S(1)} %fusion.184), slice={[0:256], [0:4096]} | slice | bytes 8388608 | tf_op jit(solution)/shard_map/slice | solution.py:180
  12.4 2.3 %copy-done = f32[512,4096]{1,0:T(8,128)} copy-done((f32[512,4096]{1,0:T(8,128)}, f32[512,4096]{1,0:T(8,128)S(1)}, u32[]{:S(2)}) %copy-start) | copy-done | bytes 8388632
  15.6 3.0 %collective-permute-start.1 = (f32[1,1024,512]{2,1,0:T(8,128)S(1)}, f32[1,1024,512]{2,1,0:T(8,128)}, u32[]{:S(2)}, u32[]{:S(2)}) collective-permute-start(f32[1,1024,512]{2,1,0:T(8,128)S(1)} %bitcast.92), channel_id=1, source_target_pairs={{0,8},{4,12},{8,0},{12,4},{1,9},{5,13},{9,1},{13,5},{2,10},{6,14},... | collective-permute-start | bytes 6291464 | tf_op jit(solution)/shard_map/ppermute | solution.py:114
  18.6 4.6 %fusion.183 = f32[512,512]{1,0:T(8,128)} fusion(f32[1024,512]{1,0:T(8,128)S(1)} %constant_dynamic-update-slice_fusion), kind=kOutput, calls=%fused_computation.310 | convolution fusion | flops 3221225472 | bytes 3145728 | tf_op jit(solution)/shard_map/ra,rb->ab/dot_general | solution.py:12
  23.4 3.5 %collective-permute-done.5 = f32[512,512]{1,0:T(8,128)} collective-permute-done((f32[512,512]{1,0:T(8,128)}, f32[512,512]{1,0:T(8,128)}, u32[]{:S(2)}, u32[]{:S(2)}) %collective-permute-start.5) | collective-permute-done | bytes 1048608 | tf_op jit(solution)/shard_map/ppermute | solution.py:114
  28.1 3.0 %collective-permute-start.6 = (f32[256,512]{1,0:T(8,128)S(1)}, f32[256,512]{1,0:T(8,128)S(1)}, u32[]{:S(2)}, u32[]{:S(2)}) collective-permute-start(f32[256,512]{1,0:T(8,128)S(1)} %dynamic-slice_add_fusion), channel_id=1, source_target_pairs={{0,1},{1,0},{2,3},{3,2},{4,5},{5,4},{6,7},{7,6},{8,9},{9,8},{10,11... | collective-permute-start | bytes 1572872 | tf_op jit(solution)/shard_map/ppermute | solution.py:141
  31.2 12.1 %collective-permute-done.6 = f32[256,512]{1,0:T(8,128)S(1)} collective-permute-done((f32[256,512]{1,0:T(8,128)S(1)}, f32[256,512]{1,0:T(8,128)S(1)}, u32[]{:S(2)}, u32[]{:S(2)}) %collective-permute-start.6) | collective-permute-done | bytes 524320 | tf_op jit(solution)/shard_map/ppermute | solution.py:141
  43.5 2.8 %collective-permute-start.7 = (f32[256,512]{1,0:T(8,128)S(1)}, f32[256,512]{1,0:T(8,128)}, u32[]{:S(2)}, u32[]{:S(2)}) collective-permute-start(f32[256,512]{1,0:T(8,128)S(1)} %add.365), channel_id=1, source_target_pairs={{0,2},{1,3},{2,0},{3,1},{4,6},{5,7},{6,4},{7,5},{8,10},{9,11},{10,... | collective-permute-start | bytes 1572872 | tf_op jit(solution)/shard_map/ppermute | solution.py:141
  46.4 18.2 %collective-permute-done.1 = f32[1,1024,512]{2,1,0:T(8,128)} collective-permute-done((f32[1,1024,512]{2,1,0:T(8,128)S(1)}, f32[1,1024,512]{2,1,0:T(8,128)}, u32[]{:S(2)}, u32[]{:S(2)}) %collective-permute-start.1) | collective-permute-done | bytes 2097184 | tf_op jit(solution)/shard_map/ppermute | solution.py:114
  64.6 3.2 %fusion.13 = f32[256,512]{1,0:T(8,128)S(1)} fusion(f32[1024,512]{1,0:T(8,128)S(1)} %constant_dynamic-update-slice_fusion, f32[256,4096]{1,0:T(8,128)} %param.6, s32[]{:T(128)S(6)} %select_n.477), kind=kOutput, calls=%fused_computation.40 | convolution fusion | flops 1610612736 | bytes 3670020 | tf_op jit(solution)/shard_map/dot_general | solution.py:8
  67.8 1.5 collective-permute-done.7
  70.4 3.5 %convolution_add_fusion = f32[256,512]{1,0:T(8,128)S(1)} fusion(f32[256,512]{1,0:T(8,128)S(1)} %fusion.13, f32[1024,512]{1,0:T(8,128)} %collective-permute-done, f32[256,4096]{1,0:T(8,128)S(1)} %copy-done.1, s32[]{:T(128)S(6)} %select_n.478), kind=kOutput, calls=%fused_computation.18 | convolution fusion | flops 1610743808 | bytes 4194308 | tf_op jit(solution)/shard_map/dot_general | solution.py:8
  74.0 3.5 %fusion.4 = f32[256,512]{1,0:T(8,128)S(1)} fusion(f32[256,512]{1,0:T(8,128)S(1)} %convolution_add_fusion, f32[1,1024,512]{2,1,0:T(8,128)} %collective-permute-done.1, f32[256,4096]{1,0:T(8,128)S(1)} %copy-done.1, s32[]{:T(128)S(6)} %select_n.479), kind=kOutput, calls=%fused_computation.16 | convolution fusion | flops 1610743808 | bytes 4194308 | tf_op jit(solution)/shard_map/dot_general | solution.py:8
  77.5 3.9 %slice_add_fusion = f32[256,4096]{1,0:T(8,128)S(1)} fusion(f32[256,4096]{1,0:T(8,128)} %collective-permute-done.8, f32[512,4096]{1,0:T(8,128)} %copy-done), kind=kLoop, calls=%fused_computation.10 | loop fusion | flops 1048576 | bytes 12582912 | tf_op jit(solution)/shard_map/add | solution.py:180
  82.9 2.1 %fusion.7 = f32[256,512]{1,0:T(8,128)S(1)} fusion(f32[256,512]{1,0:T(8,128)S(1)} %fusion.4, f32[1,1024,512]{2,1,0:T(8,128)S(1)} %collective-permute-done.2, f32[256,4096]{1,0:T(8,128)S(1)} %copy-done.1, s32[]{:T(128)S(6)} %select_n.480), kind=kOutput, calls=%fused_computation.17 | convolution fusion | flops 1610743808 | bytes 4194308 | tf_op jit(solution)/shard_map/dot_general | solution.py:8
  86.5 1.5 collective-permute-start.3
  87.9 1.5 slice.47
  90.0 6.3 %collective-permute-done.9 = f32[256,512]{1,0:T(8,128)S(1)} collective-permute-done((f32[256,512]{1,0:T(8,128)S(1)}, f32[256,512]{1,0:T(8,128)S(1)}, u32[]{:S(2)}, u32[]{:S(2)}) %collective-permute-start.9) | collective-permute-done | bytes 524320 | tf_op jit(solution)/shard_map/ppermute | solution.py:114
  97.2 5.5 %pad_maximum_fusion = f32[4,1024,512]{2,1,0:T(8,128)} fusion(f32[1,1024,512]{2,1,0:T(8,128)S(1)} %collective-permute-done.2, f32[1,1024,512]{2,1,0:T(8,128)} %collective-permute-done.1, f32[1,1024,512]{2,1,0:T(8,128)} %bitcast.11, f32[1,1024,512]{2,1,0:T(8,128)S(1)} %bitcast.93), kind=kLoop, calls=%fused_computation.7 | loop fusion | flops 6291456 | bytes 16777216 | tf_op jit(solution)/shard_map/stack | solution.py:174
  102.7 7.7 %gather_fusion.6 = f32[4,1024,512]{2,1,0:T(8,128)} fusion(f32[4,1024,512]{2,1,0:T(8,128)} %pad_maximum_fusion, s32[1024]{0:T(1024)S(1)} %pad_clamp_fusion), kind=kCustom, calls=%fused_computation.6 | custom fusion | bytes 16777232 | tf_op jit(solution)/shard_map/jit(_take)/gather | solution.py:205
  111.2 1.8 %slice_add_fusion.6 = (f32[256,256]{1,0:T(8,128)S(1)}, f32[256,256]{1,0:T(8,128)}) fusion(f32[256,256]{1,0:T(8,128)} %copy-done.7, f32[256,512]{1,0:T(8,128)S(1)} %fusion.7, f32[256,256]{1,0:T(8,128)} %collective-permute-done.3), kind=kLoop, calls=%fused_computation.306 | loop fusion | flops 131072 | bytes 1572864 | tf_op jit(solution)/shard_map/add | solution.py:141
  114.4 1.6 collective-permute-start.12
  118.0 2.3 %gather_fusion.2 = f32[256]{0:T(256)S(1)} fusion(f32[256,256]{1,0:T(8,128)S(1)} %get-tuple-element.12, s32[256]{0:T(256)S(1)} %bitcast.88), kind=kCustom, calls=%fused_computation.2 | custom fusion | bytes 4096 | tf_op jit(solution)/shard_map/jit(_diag)/jit(diagonal)/cond/branch_0_fun/gather | solution.py:99
  120.4 2.3 %gather_fusion.4 = f32[256]{0:T(256)S(1)} fusion(f32[256,256]{1,0:T(8,128)S(1)} %get-tuple-element.13, s32[256]{0:T(256)S(1)} %bitcast.89), kind=kCustom, calls=%fused_computation.4 | custom fusion | bytes 4096 | tf_op jit(solution)/shard_map/jit(_diag)/jit(diagonal)/cond/branch_0_fun/gather | solution.py:99
  122.9 2.3 %gather_fusion.3 = f32[256]{0:T(256)S(1)} fusion(f32[256,256]{1,0:T(8,128)S(1)} %get-tuple-element.10, s32[256]{0:T(256)S(1)} %bitcast.90), kind=kCustom, calls=%fused_computation.3 | custom fusion | bytes 4096 | tf_op jit(solution)/shard_map/jit(_diag)/jit(diagonal)/cond/branch_0_fun/gather | solution.py:102
  132.3 2.6 %gather_fusion.5 = f32[256]{0:T(256)S(1)} fusion(f32[256,256]{1,0:T(8,128)S(1)} %get-tuple-element.11, s32[256]{0:T(256)S(1)} %bitcast.91), kind=kCustom, calls=%fused_computation.5 | custom fusion | bytes 4096 | tf_op jit(solution)/shard_map/jit(_diag)/jit(diagonal)/cond/branch_0_fun/gather | solution.py:102
  141.7 2.0 %fusion.58 = f32[256,256]{0,1:T(8,128)S(1)} fusion(f32[256,256]{1,0:T(8,128)S(1)} %convolution_subtract_fusion.9, f32[256,256]{1,0:T(8,128)} %get-tuple-element.15, f32[256,256]{1,0:T(8,128)} %collective-permute-done.4), kind=kOutput, calls=%fused_computation.94 | convolution fusion | flops 201392128 | bytes 1048576 | tf_op jit(solution)/shard_map/dot_general | solution.py:8
  146.5 2.2 %bitcast_select_fusion = f32[4096,512]{1,0:T(8,128)S(1)} fusion(f32[4,1024,512]{2,1,0:T(8,128)S(1)} %bitcast.95, pred[4096]{0:T(1024)(128)(4,1)S(1)} %bitcast.98), kind=kLoop, calls=%fused_computation.8 | loop fusion | flops 2097152 | bytes 16781312 | tf_op jit(solution)/shard_map/jit(_take)/select_n | solution.py:205
  148.8 1.5 collective-permute-start.15
  150.3 9.0 %convolution_subtract_fusion = f32[256,4096]{1,0:T(8,128)} fusion(f32[256,4096]{1,0:T(8,128)S(1)} %copy-done.2, f32[4096,512]{1,0:T(8,128)S(1)} %bitcast_select_fusion, f32[256,256]{0,1:T(8,128)S(1)} %fusion.40, f32[256,256]{0,1:T(8,128)S(1)} %fusion.58), kind=kOutput, calls=%fused_computation.9 | convolution fusion | flops 3222405120 | bytes 17301504 | tf_op jit(solution)/shard_map/rk,ck->rc/dot_general | solution.py:32
  159.3 7.5 %add_subtract_fusion = f32[128,4096]{1,0:T(8,128)} fusion(f32[128,4096]{1,0:T(8,128)} %collective-permute-done.13, f32[256,4096]{1,0:T(8,128)S(1)} %copy-done.4, f32[4096,512]{1,0:T(8,128)S(1)} %bitcast_select_fusion, f32[128,512]{1,0:T(8,128)S(1)} %collective-permute-done.15, f32[256,512]{1,0:T(8,128)S(1)} %slice_add_fusion.1), kind=kOutput, calls=%fused_computation.15 | convolution fusion | flops 1611726848 | bytes 15204352 | tf_op jit(solution)/shard_map/rk,ck->rc/dot_general | solution.py:32
  (123 shorter events, 31.9 us)
Async XLA Ops:
  9.9 4.8 %copy-start = (f32[512,4096]{1,0:T(8,128)}, f32[512,4096]{1,0:T(8,128)S(1)}, u32[]{:S(2)}) copy-start(f32[512,4096]{1,0:T(8,128)S(1)} %fusion.184) | copy-start | bytes 25165828
  9.9 5.3 %copy-start.5 = (f32[1024,256]{1,0:T(8,128)S(1)}, f32[1024,256]{1,0:T(8,128)}, u32[]{:S(2)}) copy-start(f32[1024,256]{1,0:T(8,128)} %param.7) | copy-start | bytes 3145732
  10.0 5.4 %copy-start.6 = (f32[1024,256]{1,0:T(8,128)S(1)}, f32[1024,256]{1,0:T(8,128)}, u32[]{:S(2)}) copy-start(f32[1024,256]{1,0:T(8,128)} %param.8) | copy-start | bytes 3145732
  14.7 62.8 %collective-permute-start.8 = (f32[256,4096]{1,0:T(8,128)}, f32[256,4096]{1,0:T(8,128)}, u32[]{:S(2)}, u32[]{:S(2)}) collective-permute-start(f32[256,4096]{1,0:T(8,128)} %slice.68), channel_id=1, source_target_pairs={{0,4},{4,0},{8,12},{12,8},{1,5},{5,1},{9,13},{13,9},{2,6},{6,2},{1... | collective-permute-start | bytes 12582920 | tf_op jit(solution)/shard_map/ppermute | solution.py:114
  15.6 54.8 %collective-permute-start = (f32[1024,512]{1,0:T(8,128)S(1)}, f32[1024,512]{1,0:T(8,128)}, u32[]{:S(2)}, u32[]{:S(2)}) collective-permute-start(f32[1024,512]{1,0:T(8,128)S(1)} %constant_dynamic-update-slice_fusion), channel_id=1, source_target_pairs={{0,4},{4,0},{8,12},{12,8},{1,5},{5,1},{9,13},{13,9},{2,6},{6,2},{1... | collective-permute-start | bytes 6291464 | tf_op jit(solution)/shard_map/ppermute | solution.py:114
  15.6 48.9 %collective-permute-start.1 = (f32[1,1024,512]{2,1,0:T(8,128)S(1)}, f32[1,1024,512]{2,1,0:T(8,128)}, u32[]{:S(2)}, u32[]{:S(2)}) collective-permute-start(f32[1,1024,512]{2,1,0:T(8,128)S(1)} %bitcast.92), channel_id=1, source_target_pairs={{0,8},{4,12},{8,0},{12,4},{1,9},{5,13},{9,1},{13,5},{2,10},{6,14},... | collective-permute-start | bytes 6291464 | tf_op jit(solution)/shard_map/ppermute | solution.py:114
  23.2 3.6 %collective-permute-start.5 = (f32[512,512]{1,0:T(8,128)}, f32[512,512]{1,0:T(8,128)}, u32[]{:S(2)}, u32[]{:S(2)}) collective-permute-start(f32[512,512]{1,0:T(8,128)} %fusion.183), channel_id=1, source_target_pairs={{0,4},{4,0},{8,12},{12,8},{1,5},{5,1},{9,13},{13,9},{2,6},{6,2},{1... | collective-permute-start | bytes 3145736 | tf_op jit(solution)/shard_map/ppermute | solution.py:114
  28.1 15.2 %collective-permute-start.6 = (f32[256,512]{1,0:T(8,128)S(1)}, f32[256,512]{1,0:T(8,128)S(1)}, u32[]{:S(2)}, u32[]{:S(2)}) collective-permute-start(f32[256,512]{1,0:T(8,128)S(1)} %dynamic-slice_add_fusion), channel_id=1, source_target_pairs={{0,1},{1,0},{2,3},{3,2},{4,5},{5,4},{6,7},{7,6},{8,9},{9,8},{10,11... | collective-permute-start | bytes 1572872 | tf_op jit(solution)/shard_map/ppermute | solution.py:141
  43.5 25.8 %collective-permute-start.7 = (f32[256,512]{1,0:T(8,128)S(1)}, f32[256,512]{1,0:T(8,128)}, u32[]{:S(2)}, u32[]{:S(2)}) collective-permute-start(f32[256,512]{1,0:T(8,128)S(1)} %add.365), channel_id=1, source_target_pairs={{0,2},{1,3},{2,0},{3,1},{4,6},{5,7},{6,4},{7,5},{8,10},{9,11},{10,... | collective-permute-start | bytes 1572872 | tf_op jit(solution)/shard_map/ppermute | solution.py:141
  46.4 24.0 %copy-start.1 = (f32[256,4096]{1,0:T(8,128)S(1)}, f32[256,4096]{1,0:T(8,128)}, u32[]{:S(2)}) copy-start(f32[256,4096]{1,0:T(8,128)} %param.6) | copy-start | bytes 12582916
  64.6 18.3 %collective-permute-start.2 = (f32[1,1024,512]{2,1,0:T(8,128)}, f32[1,1024,512]{2,1,0:T(8,128)S(1)}, u32[]{:S(2)}, u32[]{:S(2)}) collective-permute-start(f32[1,1024,512]{2,1,0:T(8,128)} %collective-permute-done.1), channel_id=1, source_target_pairs={{0,4},{4,0},{8,12},{12,8},{1,5},{5,1},{9,13},{13,9},{2,6},{6,2},{1... | collective-permute-start | bytes 6291464 | tf_op jit(solution)/shard_map/ppermute | solution.py:114
  81.5 7.9 %copy-start.3 = (f32[256,4096]{1,0:T(8,128)}, f32[256,4096]{1,0:T(8,128)S(1)}, u32[]{:S(2)}) copy-start(f32[256,4096]{1,0:T(8,128)S(1)} %slice_add_fusion) | copy-start | bytes 12582916
  81.5 14.9 %collective-permute-start.9 = (f32[256,512]{1,0:T(8,128)S(1)}, f32[256,512]{1,0:T(8,128)S(1)}, u32[]{:S(2)}, u32[]{:S(2)}) collective-permute-start(f32[256,512]{1,0:T(8,128)S(1)} %add.366), channel_id=1, source_target_pairs={{0,8},{4,12},{8,0},{12,4},{1,9},{5,13},{9,1},{13,5},{2,10},{6,14},... | collective-permute-start | bytes 1572872 | tf_op jit(solution)/shard_map/ppermute | solution.py:114
  85.9 24.5 %collective-permute-start.11 = (f32[256,256]{1,0:T(8,128)}, f32[256,256]{1,0:T(8,128)S(1)}, u32[]{:S(2)}, u32[]{:S(2)}) collective-permute-start(f32[256,256]{1,0:T(8,128)} %get-tuple-element.16), channel_id=1, source_target_pairs={{0,1},{1,0},{2,3},{3,2},{4,5},{5,4},{6,7},{7,6},{8,9},{9,8},{10,11... | collective-permute-start | bytes 786440 | tf_op jit(solution)/shard_map/ppermute | solution.py:141
  86.5 24.7 %collective-permute-start.3 = (f32[256,256]{1,0:T(8,128)}, f32[256,256]{1,0:T(8,128)}, u32[]{:S(2)}, u32[]{:S(2)}) collective-permute-start(f32[256,256]{1,0:T(8,128)} %get-tuple-element.17), channel_id=1, source_target_pairs={{0,1},{1,0},{2,3},{3,2},{4,5},{5,4},{6,7},{7,6},{8,9},{9,8},{10,11... | collective-permute-start | bytes 786440 | tf_op jit(solution)/shard_map/ppermute | solution.py:141
  89.4 69.9 %collective-permute-start.13 = (f32[128,4096]{1,0:T(8,128)}, f32[128,4096]{1,0:T(8,128)}, u32[]{:S(2)}, u32[]{:S(2)}) collective-permute-start(f32[128,4096]{1,0:T(8,128)} %slice.47), channel_id=1, source_target_pairs={{0,8},{4,12},{8,0},{12,4},{1,9},{5,13},{9,1},{13,5},{2,10},{6,14},... | collective-permute-start | bytes 6291464 | tf_op jit(solution)/shard_map/ppermute | solution.py:114
  97.2 18.7 %collective-permute-start.10 = (f32[256,512]{1,0:T(8,128)}, f32[256,512]{1,0:T(8,128)}, u32[]{:S(2)}, u32[]{:S(2)}) collective-permute-start(f32[256,512]{1,0:T(8,128)} %add.369), channel_id=1, source_target_pairs={{0,4},{4,0},{8,12},{12,8},{1,5},{5,1},{9,13},{13,9},{2,6},{6,2},{1... | collective-permute-start | bytes 1572872 | tf_op jit(solution)/shard_map/ppermute | solution.py:114
  110.4 0.7 copy-start.7
  113.0 28.7 %collective-permute-start.4 = (f32[256,256]{1,0:T(8,128)}, f32[256,256]{1,0:T(8,128)}, u32[]{:S(2)}, u32[]{:S(2)}) collective-permute-start(f32[256,256]{1,0:T(8,128)} %get-tuple-element.15), channel_id=1, source_target_pairs={{0,2},{1,3},{2,0},{3,1},{4,6},{5,7},{6,4},{7,5},{8,10},{9,11},{10,... | collective-permute-start | bytes 786440 | tf_op jit(solution)/shard_map/ppermute | solution.py:141
  114.4 30.3 %collective-permute-start.12 = (f32[256,256]{1,0:T(8,128)S(1)}, f32[256,256]{1,0:T(8,128)S(1)}, u32[]{:S(2)}, u32[]{:S(2)}) collective-permute-start(f32[256,256]{1,0:T(8,128)S(1)} %get-tuple-element.14), channel_id=1, source_target_pairs={{0,2},{1,3},{2,0},{3,1},{4,6},{5,7},{6,4},{7,5},{8,10},{9,11},{10,... | collective-permute-start | bytes 786440 | tf_op jit(solution)/shard_map/ppermute | solution.py:141
  136.7 9.8 %slice-start = ((s8[8388608]{0:T(1024)(128)(4,1)}), s8[4194304]{0:T(1024)(128)(4,1)S(1)}, s32[]{:S(2)}) async-start(s8[8388608]{0:T(1024)(128)(4,1)} %bitcast.94), calls=%async_computation | async-start | bytes 8388608
  140.8 5.7 %slice-start.1 = ((s8[8388608]{0:T(1024)(128)(4,1)}), s8[4194304]{0:T(1024)(128)(4,1)S(1)}, s32[]{:S(2)}) async-start(s8[8388608]{0:T(1024)(128)(4,1)} %bitcast.94), calls=%async_computation.1 | async-start | bytes 8388608
  146.4 2.3 %collective-permute-start.14 = (f32[256,512]{1,0:T(8,128)S(1)}, f32[256,512]{1,0:T(8,128)S(1)}, u32[]{:S(2)}, u32[]{:S(2)}) collective-permute-start(f32[256,512]{1,0:T(8,128)S(1)} %slice.74), channel_id=1, source_target_pairs={{0,4},{4,0},{8,12},{12,8},{1,5},{5,1},{9,13},{13,9},{2,6},{6,2},{1... | collective-permute-start | bytes 1572872 | tf_op jit(solution)/shard_map/ppermute | solution.py:114
  146.5 3.8 %copy-start.2 = (f32[256,4096]{1,0:T(8,128)S(1)}, f32[256,4096]{1,0:T(8,128)}, u32[]{:S(2)}) copy-start(f32[256,4096]{1,0:T(8,128)} %param.6) | copy-start | bytes 12582916
  148.8 10.5 %copy-start.4 = (f32[256,4096]{1,0:T(8,128)S(1)}, f32[256,4096]{1,0:T(8,128)}, u32[]{:S(2)}) copy-start(f32[256,4096]{1,0:T(8,128)} %copy-done.3) | copy-start | bytes 12582916
  148.8 10.5 %collective-permute-start.15 = (f32[128,512]{1,0:T(8,128)S(1)}, f32[128,512]{1,0:T(8,128)S(1)}, u32[]{:S(2)}, u32[]{:S(2)}) collective-permute-start(f32[128,512]{1,0:T(8,128)S(1)} %slice.76), channel_id=1, source_target_pairs={{0,8},{4,12},{8,0},{12,4},{1,9},{5,13},{9,1},{13,5},{2,10},{6,14},... | collective-permute-start | bytes 786440 | tf_op jit(solution)/shard_map/ppermute | solution.py:114

commit v3 on v2

--- a/solution.py
+++ b/solution.py
@@ -200,7 +200,10 @@
         cols = lax.dynamic_slice_in_dim(basis, (me ^ slot) * span, span, axis=1)
         part = dot_high(cols, held[slot])
         image = part if image is None else image + part
-    image = jnp.concatenate([col_sum(image[:, :k]), col_sum(image[:, k:])], axis=1)
+    quarter = k // 2
+    image = jnp.concatenate(
+        [col_sum(image[:, at : at + quarter]) for at in range(0, 2 * k, quarter)], axis=1
+    )
 
     gathered = jnp.take(held, jnp.arange(size) ^ me, axis=0).reshape(size * span, -1)
     factor_one = tri_factor_doubling(gram[:k, :k])

time: 170 us -> 188 us (1.11)
  other arithmetic: 19.4 us -> 35.7 us
  waiting for transfers between devices: 41.6 us -> 36.5 us
  local copies, waits for them, and re-layouts: 28.6 us -> 33.3 us
  starting transfers between devices: 17.9 us -> 21 us
    ppermute x10, waiting for transfers between devices: 27.9 us -> 21.1 us  [swap(): return lax.ppermute(value, 'row', [(i, i ^ distance) for i in range(size)])]
    ppermute x6 -> x10, starting transfers between devices: 10.8 us -> 14.2 us  [col_sum(): lax.ppermute(value, 'col', [(i, i ^ distance) for i in range(size)])]
    add x3 -> x7, other arithmetic: 3.07 us -> 6.15 us  [col_sum(): value + lax.ppermute(value, 'col', [(i, i ^ distance) for i in range(size)])]
    unnamed x24 -> x82, local copies, waits for them, and re-layouts: 4.53 us -> 7.04 us
    eq x4, other arithmetic: 0.03 us -> 2.24 us  [tri_factor_doubling(): side[None, :] == 1]
    eq x4, other arithmetic: 0.03 us -> 2.24 us  [tri_factor_doubling(): side[:, None] == 0]
    add x1, other arithmetic: 3.95 us -> 6.11 us  [shards(): head = head[count:] + swap(head[:count], 1, size)]
    ppermute x6 -> x10, waiting for transfers between devices: 13.6 us -> 15.4 us  [col_sum(): lax.ppermute(value, 'col', [(i, i ^ distance) for i in range(size)])]
  transfers between devices with their start and end apart: 16 -> 20, of which waited for: 5 -> 8; matrix products, arithmetic and copies ran while one was open for 50% -> 56% of each run, Pallas kernels for 0% -> 0%
where the time goes in v3:
time: 188 us; the launch traced here: 185 us
  matrix products  56.1 us (30%)
  waiting for transfers between devices  36.5 us (19%)
  other arithmetic  35.7 us (19%)
  local copies, waits for them, and re-layouts  33.3 us (18%)
  starting transfers between devices  21 us (11%)
  between operations  1.91 us (1%)
    dot_general x39, matrix products, dot_high(): jnp.dot(left, right, precision=lax.Precision.HIGHEST, preferred_element_t...  28.2 us
    ppermute x10, waiting for transfers between devices, swap(): return lax.ppermute(value, 'row', [(i, i ^ distance) for i in range(size)])  21.1 us
    dot_general x2, matrix products, outer_mid(): jnp.einsum('rk,ck->rc', left, right, precision=lax.Precision.HIGH, prefer...  16.4 us
    ppermute x10, waiting for transfers between devices, col_sum(): lax.ppermute(value, 'col', [(i, i ^ distance) for i in range(size)])  15.4 us
    ppermute x10, starting transfers between devices, col_sum(): lax.ppermute(value, 'col', [(i, i ^ distance) for i in range(size)])  14.2 us
    gather x1, local copies, waits for them, and re-layouts, shards(): jnp.take(held, jnp.arange(size) ^ me, axis=0).reshape(size * span, -1)  7.92 us
    unnamed x82, local copies, waits for them, and re-layouts  7.04 us
    ppermute x10, starting transfers between devices, swap(): return lax.ppermute(value, 'row', [(i, i ^ distance) for i in range(size)])  6.81 us
  transfers between devices with their start and end apart: 20, of which 8 were waited for; matrix products, arithmetic and copies ran while one was open for 56% of the time, Pallas kernels for 0%

profile of v3, /device:TPU:0, one launch (start us, length us, event | category | flops | bytes accessed | tf_op | source)
XLA Modules:
  0.0 184.6 jit_solution(15021177082933654774)
XLA Ops:
  3.8 5.8 %fusion.188 = f32[512,4096]{1,0:T(8,128)S(1)} fusion(f32[256,512]{0,1:T(8,128)S(1)} %bitcast_select_fusion.2, f32[256,4096]{1,0:T(8,128)} %param.6), kind=kOutput, calls=%fused_computation.318 | convolution fusion | flops 3221225472 | bytes 13107200 | tf_op jit(solution)/shard_map/ra,rb->ab/dot_general | solution.py:42
  9.6 2.5 %slice.81 = f32[256,4096]{1,0:T(8,128)} slice(f32[512,4096]{1,0:T(8,128)S(1)} %fusion.188), slice={[0:256], [0:4096]} | slice | bytes 8388608 | tf_op jit(solution)/shard_map/slice | solution.py:180
  12.1 2.3 %copy-done = f32[512,4096]{1,0:T(8,128)} copy-done((f32[512,4096]{1,0:T(8,128)}, f32[512,4096]{1,0:T(8,128)S(1)}, u32[]{:S(2)}) %copy-start) | copy-done | bytes 8388632
  15.3 3.0 %collective-permute-start.1 = (f32[1,1024,512]{2,1,0:T(8,128)S(1)}, f32[1,1024,512]{2,1,0:T(8,128)}, u32[]{:S(2)}, u32[]{:S(2)}) collective-permute-start(f32[1,1024,512]{2,1,0:T(8,128)S(1)} %bitcast.92), channel_id=1, source_target_pairs={{0,8},{4,12},{8,0},{12,4},{1,9},{5,13},{9,1},{13,5},{2,10},{6,14},... | collective-permute-start | bytes 6291464 | tf_op jit(solution)/shard_map/ppermute | solution.py:114
  18.3 4.6 %fusion.187 = f32[512,512]{1,0:T(8,128)} fusion(f32[1024,512]{1,0:T(8,128)S(1)} %constant_dynamic-update-slice_fusion), kind=kOutput, calls=%fused_computation.317 | convolution fusion | flops 3221225472 | bytes 3145728 | tf_op jit(solution)/shard_map/ra,rb->ab/dot_general | solution.py:12
  29.2 1.6 collective-permute-start.8
  32.6 11.0 %collective-permute-done.8 = f32[256,512]{1,0:T(8,128)S(1)} collective-permute-done((f32[256,512]{1,0:T(8,128)S(1)}, f32[256,512]{1,0:T(8,128)S(1)}, u32[]{:S(2)}, u32[]{:S(2)}) %collective-permute-start.8) | collective-permute-done | bytes 524320 | tf_op jit(solution)/shard_map/ppermute | solution.py:141
  43.7 2.7 %collective-permute-start.9 = (f32[256,512]{1,0:T(8,128)S(1)}, f32[256,512]{1,0:T(8,128)}, u32[]{:S(2)}, u32[]{:S(2)}) collective-permute-start(f32[256,512]{1,0:T(8,128)S(1)} %add.379), channel_id=1, source_target_pairs={{0,2},{1,3},{2,0},{3,1},{4,6},{5,7},{6,4},{7,5},{8,10},{9,11},{10,... | collective-permute-start | bytes 1572872 | tf_op jit(solution)/shard_map/ppermute | solution.py:141
  47.5 16.7 %collective-permute-done.1 = f32[1,1024,512]{2,1,0:T(8,128)} collective-permute-done((f32[1,1024,512]{2,1,0:T(8,128)S(1)}, f32[1,1024,512]{2,1,0:T(8,128)}, u32[]{:S(2)}, u32[]{:S(2)}) %collective-permute-start.1) | collective-permute-done | bytes 2097184 | tf_op jit(solution)/shard_map/ppermute | solution.py:114
  64.2 3.2 %fusion.13 = f32[256,512]{1,0:T(8,128)S(1)} fusion(f32[1024,512]{1,0:T(8,128)S(1)} %constant_dynamic-update-slice_fusion, f32[256,4096]{1,0:T(8,128)} %param.6, s32[]{:T(128)S(6)} %select_n.477), kind=kOutput, calls=%fused_computation.40 | convolution fusion | flops 1610612736 | bytes 3670020 | tf_op jit(solution)/shard_map/dot_general | solution.py:8
  67.4 2.1 %collective-permute-done.9 = f32[256,512]{1,0:T(8,128)} collective-permute-done((f32[256,512]{1,0:T(8,128)S(1)}, f32[256,512]{1,0:T(8,128)}, u32[]{:S(2)}, u32[]{:S(2)}) %collective-permute-start.9) | collective-permute-done | bytes 524320 | tf_op jit(solution)/shard_map/ppermute | solution.py:141
  69.6 2.0 %add.380 = f32[256,512]{1,0:T(8,128)} add(f32[256,512]{1,0:T(8,128)S(1)} %add.379, f32[256,512]{1,0:T(8,128)} %collective-permute-done.9) | non-fusion elementwise | flops 131072 | bytes 1572864 | tf_op jit(solution)/shard_map/add | solution.py:141
  71.5 3.5 %convolution_add_fusion = f32[256,512]{1,0:T(8,128)S(1)} fusion(f32[256,512]{1,0:T(8,128)S(1)} %fusion.13, f32[1024,512]{1,0:T(8,128)} %collective-permute-done, f32[256,4096]{1,0:T(8,128)S(1)} %copy-done.1, s32[]{:T(128)S(6)} %select_n.478), kind=kOutput, calls=%fused_computation.18 | convolution fusion | flops 1610743808 | bytes 4194308 | tf_op jit(solution)/shard_map/dot_general | solution.py:8
  75.1 3.6 %fusion.4 = f32[256,512]{1,0:T(8,128)S(1)} fusion(f32[256,512]{1,0:T(8,128)S(1)} %convolution_add_fusion, f32[1,1024,512]{2,1,0:T(8,128)} %collective-permute-done.1, f32[256,4096]{1,0:T(8,128)S(1)} %copy-done.1, s32[]{:T(128)S(6)} %select_n.479), kind=kOutput, calls=%fused_computation.16 | convolution fusion | flops 1610743808 | bytes 4194308 | tf_op jit(solution)/shard_map/dot_general | solution.py:8
  78.7 6.1 %slice_add_fusion = f32[256,4096]{1,0:T(8,128)} fusion(f32[256,4096]{1,0:T(8,128)} %collective-permute-done.10, f32[512,4096]{1,0:T(8,128)} %copy-done), kind=kLoop, calls=%fused_computation.10 | loop fusion | flops 1048576 | bytes 12582912 | tf_op jit(solution)/shard_map/add | solution.py:180
  85.5 2.2 %fusion.7 = f32[256,512]{1,0:T(8,128)S(1)} fusion(f32[256,512]{1,0:T(8,128)S(1)} %fusion.4, f32[1,1024,512]{2,1,0:T(8,128)S(1)} %collective-permute-done.2, f32[256,4096]{1,0:T(8,128)S(1)} %copy-done.1, s32[]{:T(128)S(6)} %select_n.480), kind=kOutput, calls=%fused_computation.17 | convolution fusion | flops 1610743808 | bytes 4194308 | tf_op jit(solution)/shard_map/dot_general | solution.py:8
  97.9 2.1 %add.383 = f32[256,512]{1,0:T(8,128)} add(f32[256,512]{1,0:T(8,128)} %add.380, f32[256,512]{1,0:T(8,128)} %collective-permute-done.11) | non-fusion elementwise | flops 131072 | bytes 1572864 | tf_op jit(solution)/shard_map/add | solution.py:189
  101.7 1.8 slice_add_fusion.7
  103.6 2.9 %collective-permute-start.14 = (f32[256,128]{1,0:T(8,128)}, f32[256,128]{1,0:T(8,128)S(1)}, u32[]{:S(2)}, u32[]{:S(2)}) collective-permute-start(f32[256,128]{1,0:T(8,128)} %get-tuple-element.14), channel_id=1, source_target_pairs={{0,2},{1,3},{2,0},{3,1},{4,6},{5,7},{6,4},{7,5},{8,10},{9,11},{10,... | collective-permute-start | bytes 393224 | tf_op jit(solution)/shard_map/ppermute | solution.py:141
  106.5 2.9 %collective-permute-start.4 = (f32[256,128]{1,0:T(8,128)S(1)}, f32[256,128]{1,0:T(8,128)S(1)}, u32[]{:S(2)}, u32[]{:S(2)}) collective-permute-start(f32[256,128]{1,0:T(8,128)S(1)} %get-tuple-element.15), channel_id=1, source_target_pairs={{0,2},{1,3},{2,0},{3,1},{4,6},{5,7},{6,4},{7,5},{8,10},{9,11},{10,... | collective-permute-start | bytes 393224 | tf_op jit(solution)/shard_map/ppermute | solution.py:141
  109.4 5.7 %pad_maximum_fusion = f32[4,1024,512]{2,1,0:T(8,128)} fusion(f32[1,1024,512]{2,1,0:T(8,128)S(1)} %copy-done.6, f32[1,1024,512]{2,1,0:T(8,128)} %collective-permute-done.1, f32[1,1024,512]{2,1,0:T(8,128)} %bitcast.11, f32[1,1024,512]{2,1,0:T(8,128)S(1)} %bitcast.93), kind=kLoop, calls=%fused_computation.7 | loop fusion | flops 6291456 | bytes 16777216 | tf_op jit(solution)/shard_map/stack | solution.py:174
  116.7 7.9 %gather_fusion.6 = f32[4,1024,512]{2,1,0:T(8,128)} fusion(f32[4,1024,512]{2,1,0:T(8,128)} %pad_maximum_fusion, s32[1024]{0:T(1024)} %pad_clamp_fusion), kind=kCustom, calls=%fused_computation.6 | custom fusion | bytes 16777232 | tf_op jit(solution)/shard_map/jit(_take)/gather | solution.py:208
  125.9 1.6 add.394
  128.2 1.7 collective-permute-done.6
  132.8 2.3 %gather_fusion.2 = f32[256]{0:T(256)S(1)} fusion(f32[256,256]{1,0:T(8,128)S(1)} %get-tuple-element.12, s32[256]{0:T(256)S(1)} %bitcast.88), kind=kCustom, calls=%fused_computation.2 | custom fusion | bytes 4096 | tf_op jit(solution)/shard_map/jit(_diag)/jit(diagonal)/cond/branch_0_fun/gather | solution.py:99
  135.2 2.3 %gather_fusion.4 = f32[256]{0:T(256)S(1)} fusion(f32[256,256]{1,0:T(8,128)S(1)} %get-tuple-element.13, s32[256]{0:T(256)S(1)} %bitcast.89), kind=kCustom, calls=%fused_computation.4 | custom fusion | bytes 4096 | tf_op jit(solution)/shard_map/jit(_diag)/jit(diagonal)/cond/branch_0_fun/gather | solution.py:99
  137.7 2.3 %gather_fusion.3 = f32[256]{0:T(256)S(1)} fusion(f32[256,256]{1,0:T(8,128)S(1)} %get-tuple-element.10, s32[256]{0:T(256)S(1)} %bitcast.90), kind=kCustom, calls=%fused_computation.3 | custom fusion | bytes 4096 | tf_op jit(solution)/shard_map/jit(_diag)/jit(diagonal)/cond/branch_0_fun/gather | solution.py:102
  148.7 2.7 %gather_fusion.5 = f32[256]{0:T(256)S(1)} fusion(f32[256,256]{1,0:T(8,128)S(1)} %get-tuple-element.11, s32[256]{0:T(256)S(1)} %bitcast.91), kind=kCustom, calls=%fused_computation.5 | custom fusion | bytes 4096 | tf_op jit(solution)/shard_map/jit(_diag)/jit(diagonal)/cond/branch_0_fun/gather | solution.py:102
  160.5 2.2 %bitcast_select_fusion = f32[4096,512]{1,0:T(8,128)S(1)} fusion(f32[4,1024,512]{2,1,0:T(8,128)S(1)} %bitcast.95, pred[4096]{0:T(1024)(128)(4,1)S(1)} %bitcast.98), kind=kLoop, calls=%fused_computation.8 | loop fusion | flops 2097152 | bytes 16781312 | tf_op jit(solution)/shard_map/jit(_take)/select_n | solution.py:208
  164.0 8.9 %convolution_subtract_fusion = f32[256,4096]{1,0:T(8,128)} fusion(f32[256,4096]{1,0:T(8,128)S(1)} %copy-done.2, f32[4096,512]{1,0:T(8,128)S(1)} %bitcast_select_fusion, f32[256,256]{0,1:T(8,128)S(1)} %fusion.29, f32[256,256]{0,1:T(8,128)S(1)} %fusion.25), kind=kOutput, calls=%fused_computation.9 | convolution fusion | flops 3222405120 | bytes 17301504 | tf_op jit(solution)/shard_map/rk,ck->rc/dot_general | solution.py:32
  172.9 4.0 %collective-permute-done.19 = f32[128,512]{1,0:T(8,128)S(1)} collective-permute-done((f32[128,512]{1,0:T(8,128)S(1)}, f32[128,512]{1,0:T(8,128)S(1)}, u32[]{:S(2)}, u32[]{:S(2)}) %collective-permute-start.19) | collective-permute-done | bytes 262176 | tf_op jit(solution)/shard_map/ppermute | solution.py:114
  176.9 7.5 %add_subtract_fusion = f32[128,4096]{1,0:T(8,128)} fusion(f32[128,4096]{1,0:T(8,128)} %collective-permute-done.17, f32[256,4096]{1,0:T(8,128)S(1)} %copy-done.4, f32[4096,512]{1,0:T(8,128)S(1)} %bitcast_select_fusion, f32[128,512]{1,0:T(8,128)S(1)} %collective-permute-done.19, f32[256,512]{1,0:T(8,128)S(1)} %slice_add_fusion.1), kind=kOutput, calls=%fused_computation.15 | convolution fusion | flops 1611726848 | bytes 15204352 | tf_op jit(solution)/shard_map/rk,ck->rc/dot_general | solution.py:32
  (193 shorter events, 50.8 us)
Async XLA Ops:
  14.4 64.2 %collective-permute-start.10 = (f32[256,4096]{1,0:T(8,128)}, f32[256,4096]{1,0:T(8,128)}, u32[]{:S(2)}, u32[]{:S(2)}) collective-permute-start(f32[256,4096]{1,0:T(8,128)} %slice.81), channel_id=1, source_target_pairs={{0,4},{4,0},{8,12},{12,8},{1,5},{5,1},{9,13},{13,9},{2,6},{6,2},{1... | collective-permute-start | bytes 12582920 | tf_op jit(solution)/shard_map/ppermute | solution.py:114
  15.2 56.3 %collective-permute-start = (f32[1024,512]{1,0:T(8,128)S(1)}, f32[1024,512]{1,0:T(8,128)}, u32[]{:S(2)}, u32[]{:S(2)}) collective-permute-start(f32[1024,512]{1,0:T(8,128)S(1)} %constant_dynamic-update-slice_fusion), channel_id=1, source_target_pairs={{0,4},{4,0},{8,12},{12,8},{1,5},{5,1},{9,13},{13,9},{2,6},{6,2},{1... | collective-permute-start | bytes 6291464 | tf_op jit(solution)/shard_map/ppermute | solution.py:114
  15.3 48.9 %collective-permute-start.1 = (f32[1,1024,512]{2,1,0:T(8,128)S(1)}, f32[1,1024,512]{2,1,0:T(8,128)}, u32[]{:S(2)}, u32[]{:S(2)}) collective-permute-start(f32[1,1024,512]{2,1,0:T(8,128)S(1)} %bitcast.92), channel_id=1, source_target_pairs={{0,8},{4,12},{8,0},{12,4},{1,9},{5,13},{9,1},{13,5},{2,10},{6,14},... | collective-permute-start | bytes 6291464 | tf_op jit(solution)/shard_map/ppermute | solution.py:114
  22.9 5.1 %collective-permute-start.7 = (f32[512,512]{1,0:T(8,128)}, f32[512,512]{1,0:T(8,128)}, u32[]{:S(2)}, u32[]{:S(2)}) collective-permute-start(f32[512,512]{1,0:T(8,128)} %fusion.187), channel_id=1, source_target_pairs={{0,4},{4,0},{8,12},{12,8},{1,5},{5,1},{9,13},{13,9},{2,6},{6,2},{1... | collective-permute-start | bytes 3145736 | tf_op jit(solution)/shard_map/ppermute | solution.py:114
  29.2 14.4 %collective-permute-start.8 = (f32[256,512]{1,0:T(8,128)S(1)}, f32[256,512]{1,0:T(8,128)S(1)}, u32[]{:S(2)}, u32[]{:S(2)}) collective-permute-start(f32[256,512]{1,0:T(8,128)S(1)} %dynamic-slice_add_fusion), channel_id=1, source_target_pairs={{0,1},{1,0},{2,3},{3,2},{4,5},{5,4},{6,7},{7,6},{8,9},{9,8},{10,11... | collective-permute-start | bytes 1572872 | tf_op jit(solution)/shard_map/ppermute | solution.py:141
  43.7 25.9 %collective-permute-start.9 = (f32[256,512]{1,0:T(8,128)S(1)}, f32[256,512]{1,0:T(8,128)}, u32[]{:S(2)}, u32[]{:S(2)}) collective-permute-start(f32[256,512]{1,0:T(8,128)S(1)} %add.379), channel_id=1, source_target_pairs={{0,2},{1,3},{2,0},{3,1},{4,6},{5,7},{6,4},{7,5},{8,10},{9,11},{10,... | collective-permute-start | bytes 1572872 | tf_op jit(solution)/shard_map/ppermute | solution.py:141
  46.9 24.7 %copy-start.1 = (f32[256,4096]{1,0:T(8,128)S(1)}, f32[256,4096]{1,0:T(8,128)}, u32[]{:S(2)}) copy-start(f32[256,4096]{1,0:T(8,128)} %param.6) | copy-start | bytes 12582916
  64.2 21.2 %collective-permute-start.2 = (f32[1,1024,512]{2,1,0:T(8,128)}, f32[1,1024,512]{2,1,0:T(8,128)S(1)}, u32[]{:S(2)}, u32[]{:S(2)}) collective-permute-start(f32[1,1024,512]{2,1,0:T(8,128)} %collective-permute-done.1), channel_id=1, source_target_pairs={{0,4},{4,0},{8,12},{12,8},{1,5},{5,1},{9,13},{13,9},{2,6},{6,2},{1... | collective-permute-start | bytes 6291464 | tf_op jit(solution)/shard_map/ppermute | solution.py:114
  84.8 13.2 %collective-permute-start.11 = (f32[256,512]{1,0:T(8,128)}, f32[256,512]{1,0:T(8,128)}, u32[]{:S(2)}, u32[]{:S(2)}) collective-permute-start(f32[256,512]{1,0:T(8,128)} %add.380), channel_id=1, source_target_pairs={{0,8},{4,12},{8,0},{12,4},{1,9},{5,13},{9,1},{13,5},{2,10},{6,14},... | collective-permute-start | bytes 1572872 | tf_op jit(solution)/shard_map/ppermute | solution.py:114
  88.5 11.5 %collective-permute-start.13 = (f32[256,128]{1,0:T(8,128)}, f32[256,128]{1,0:T(8,128)S(1)}, u32[]{:S(2)}, u32[]{:S(2)}) collective-permute-start(f32[256,128]{1,0:T(8,128)} %get-tuple-element.18), channel_id=1, source_target_pairs={{0,1},{1,0},{2,3},{3,2},{4,5},{5,4},{6,7},{7,6},{8,9},{9,8},{10,11... | collective-permute-start | bytes 393224 | tf_op jit(solution)/shard_map/ppermute | solution.py:141
  89.0 11.0 %collective-permute-start.15 = (f32[256,128]{1,0:T(8,128)}, f32[256,128]{1,0:T(8,128)S(1)}, u32[]{:S(2)}, u32[]{:S(2)}) collective-permute-start(f32[256,128]{1,0:T(8,128)} %get-tuple-element.19), channel_id=1, source_target_pairs={{0,1},{1,0},{2,3},{3,2},{4,5},{5,4},{6,7},{7,6},{8,9},{9,8},{10,11... | collective-permute-start | bytes 393224 | tf_op jit(solution)/shard_map/ppermute | solution.py:141
  90.5 9.7 %collective-permute-start.3 = (f32[256,128]{1,0:T(8,128)}, f32[256,128]{1,0:T(8,128)S(1)}, u32[]{:S(2)}, u32[]{:S(2)}) collective-permute-start(f32[256,128]{1,0:T(8,128)} %get-tuple-element.21), channel_id=1, source_target_pairs={{0,1},{1,0},{2,3},{3,2},{4,5},{5,4},{6,7},{7,6},{8,9},{9,8},{10,11... | collective-permute-start | bytes 393224 | tf_op jit(solution)/shard_map/ppermute | solution.py:141
  91.1 10.7 %collective-permute-start.5 = (f32[256,128]{1,0:T(8,128)}, f32[256,128]{1,0:T(8,128)}, u32[]{:S(2)}, u32[]{:S(2)}) collective-permute-start(f32[256,128]{1,0:T(8,128)} %get-tuple-element.20), channel_id=1, source_target_pairs={{0,1},{1,0},{2,3},{3,2},{4,5},{5,4},{6,7},{7,6},{8,9},{9,8},{10,11... | collective-permute-start | bytes 393224 | tf_op jit(solution)/shard_map/ppermute | solution.py:141
  94.9 14.5 %copy-start.6 = (f32[1,1024,512]{2,1,0:T(8,128)S(1)}, f32[1,1024,512]{2,1,0:T(8,128)}, u32[]{:S(2)}) copy-start(f32[1,1024,512]{2,1,0:T(8,128)} %copy-done.5) | copy-start | bytes 6291460
  100.0 29.9 %collective-permute-start.12 = (f32[256,512]{1,0:T(8,128)}, f32[256,512]{1,0:T(8,128)}, u32[]{:S(2)}, u32[]{:S(2)}) collective-permute-start(f32[256,512]{1,0:T(8,128)} %add.383), channel_id=1, source_target_pairs={{0,4},{4,0},{8,12},{12,8},{1,5},{5,1},{9,13},{13,9},{2,6},{6,2},{1... | collective-permute-start | bytes 1572872 | tf_op jit(solution)/shard_map/ppermute | solution.py:114
  103.6 21.0 %collective-permute-start.14 = (f32[256,128]{1,0:T(8,128)}, f32[256,128]{1,0:T(8,128)S(1)}, u32[]{:S(2)}, u32[]{:S(2)}) collective-permute-start(f32[256,128]{1,0:T(8,128)} %get-tuple-element.14), channel_id=1, source_target_pairs={{0,2},{1,3},{2,0},{3,1},{4,6},{5,7},{6,4},{7,5},{8,10},{9,11},{10,... | collective-permute-start | bytes 393224 | tf_op jit(solution)/shard_map/ppermute | solution.py:141
  106.5 21.0 %collective-permute-start.16 = (f32[256,128]{1,0:T(8,128)S(1)}, f32[256,128]{1,0:T(8,128)S(1)}, u32[]{:S(2)}, u32[]{:S(2)}) collective-permute-start(f32[256,128]{1,0:T(8,128)S(1)} %get-tuple-element.17), channel_id=1, source_target_pairs={{0,2},{1,3},{2,0},{3,1},{4,6},{5,7},{6,4},{7,5},{8,10},{9,11},{10,... | collective-permute-start | bytes 393224 | tf_op jit(solution)/shard_map/ppermute | solution.py:141
  106.5 21.6 %collective-permute-start.4 = (f32[256,128]{1,0:T(8,128)S(1)}, f32[256,128]{1,0:T(8,128)S(1)}, u32[]{:S(2)}, u32[]{:S(2)}) collective-permute-start(f32[256,128]{1,0:T(8,128)S(1)} %get-tuple-element.15), channel_id=1, source_target_pairs={{0,2},{1,3},{2,0},{3,1},{4,6},{5,7},{6,4},{7,5},{8,10},{9,11},{10,... | collective-permute-start | bytes 393224 | tf_op jit(solution)/shard_map/ppermute | solution.py:141
  109.4 20.4 %collective-permute-start.6 = (f32[256,128]{1,0:T(8,128)S(1)}, f32[256,128]{1,0:T(8,128)S(1)}, u32[]{:S(2)}, u32[]{:S(2)}) collective-permute-start(f32[256,128]{1,0:T(8,128)S(1)} %get-tuple-element.16), channel_id=1, source_target_pairs={{0,2},{1,3},{2,0},{3,1},{4,6},{5,7},{6,4},{7,5},{8,10},{9,11},{10,... | collective-permute-start | bytes 393224 | tf_op jit(solution)/shard_map/ppermute | solution.py:141
  124.6 52.3 %collective-permute-start.17 = (f32[128,4096]{1,0:T(8,128)}, f32[128,4096]{1,0:T(8,128)}, u32[]{:S(2)}, u32[]{:S(2)}) collective-permute-start(f32[128,4096]{1,0:T(8,128)} %slice.59), channel_id=1, source_target_pairs={{0,8},{4,12},{8,0},{12,4},{1,9},{5,13},{9,1},{13,5},{2,10},{6,14},... | collective-permute-start | bytes 6291464 | tf_op jit(solution)/shard_map/ppermute | solution.py:114
  131.9 9.1 %copy-start.15 = (s32[256]{0:T(256)S(1)}, s32[256]{0:T(256)}, u32[]{:S(2)}) copy-start(s32[256]{0:T(256)} %get-tuple-element.29) | copy-start | bytes 3076
  131.9 9.1 %copy-start.30 = (pred[256]{0:T(512)(128)(4,1)S(1)}, pred[256]{0:T(512)(128)(4,1)}, u32[]{:S(2)}) copy-start(pred[256]{0:T(512)(128)(4,1)} %get-tuple-element.45) | copy-start | bytes 772
  132.0 9.1 %copy-start.32 = (pred[256]{0:T(512)(128)(4,1)S(1)}, pred[256]{0:T(512)(128)(4,1)}, u32[]{:S(2)}) copy-start(pred[256]{0:T(512)(128)(4,1)} %get-tuple-element.35) | copy-start | bytes 772
  132.7 9.3 %copy-start.17 = (s32[256]{0:T(256)S(1)}, s32[256]{0:T(256)}, u32[]{:S(2)}) copy-start(s32[256]{0:T(256)} %get-tuple-element.28) | copy-start | bytes 3076
  132.7 9.3 %copy-start.29 = (pred[256]{0:T(512)(128)(4,1)S(1)}, pred[256]{0:T(512)(128)(4,1)}, u32[]{:S(2)}) copy-start(pred[256]{0:T(512)(128)(4,1)} %get-tuple-element.34) | copy-start | bytes 772
  132.7 9.3 %copy-start.31 = (pred[256]{0:T(512)(128)(4,1)S(1)}, pred[256]{0:T(512)(128)(4,1)}, u32[]{:S(2)}) copy-start(pred[256]{0:T(512)(128)(4,1)} %get-tuple-element.44) | copy-start | bytes 772
  132.8 10.1 %copy-start.16 = (s32[256]{0:T(256)S(1)}, s32[256]{0:T(256)}, u32[]{:S(2)}) copy-start(s32[256]{0:T(256)} %get-tuple-element.27) | copy-start | bytes 3076
  132.8 10.1 %copy-start.26 = (pred[256]{0:T(512)(128)(4,1)S(1)}, pred[256]{0:T(512)(128)(4,1)}, u32[]{:S(2)}) copy-start(pred[256]{0:T(512)(128)(4,1)} %get-tuple-element.33) | copy-start | bytes 772
  132.8 10.1 %copy-start.28 = (pred[256]{0:T(512)(128)(4,1)S(1)}, pred[256]{0:T(512)(128)(4,1)}, u32[]{:S(2)}) copy-start(pred[256]{0:T(512)(128)(4,1)} %get-tuple-element.43) | copy-start | bytes 772
  160.3 2.3 %collective-permute-start.18 = (f32[256,512]{1,0:T(8,128)S(1)}, f32[256,512]{1,0:T(8,128)S(1)}, u32[]{:S(2)}, u32[]{:S(2)}) collective-permute-start(f32[256,512]{1,0:T(8,128)S(1)} %slice.88), channel_id=1, source_target_pairs={{0,4},{4,0},{8,12},{12,8},{1,5},{5,1},{9,13},{13,9},{2,6},{6,2},{1... | collective-permute-start | bytes 1572872 | tf_op jit(solution)/shard_map/ppermute | solution.py:114
  162.8 14.1 %copy-start.4 = (f32[256,4096]{1,0:T(8,128)S(1)}, f32[256,4096]{1,0:T(8,128)}, u32[]{:S(2)}) copy-start(f32[256,4096]{1,0:T(8,128)} %slice_add_fusion) | copy-start | bytes 12582916
  162.8 14.1 %collective-permute-start.19 = (f32[128,512]{1,0:T(8,128)S(1)}, f32[128,512]{1,0:T(8,128)S(1)}, u32[]{:S(2)}, u32[]{:S(2)}) collective-permute-start(f32[128,512]{1,0:T(8,128)S(1)} %slice.90), channel_id=1, source_target_pairs={{0,8},{4,12},{8,0},{12,4},{1,9},{5,13},{9,1},{13,5},{2,10},{6,14},... | collective-permute-start | bytes 786440 | tf_op jit(solution)/shard_map/ppermute | solution.py:114
  (27 other events, 140.5 us)

commit v4 on v2

--- a/solution.py
+++ b/solution.py
@@ -183,7 +183,8 @@
     gram_chip = gram_own + swap(gram_own, 1, size)
     half = me % 2
     rows = gram_chip.shape[0] // 2
-    mine = col_sum(lax.dynamic_slice_in_dim(gram_chip, half * rows, rows, axis=0))
+    mine = lax.dynamic_slice_in_dim(gram_chip, half * rows, rows, axis=0)
+    mine = jnp.concatenate([col_sum(mine[:, :k]), col_sum(mine[:, k:])], axis=1)
     mine, head = lax.optimization_barrier((mine, head))
     for distance in spread(size)[1:]:
         mine = mine + swap(mine, distance, size)

time: 170 us -> 175 us (1.029)
  local copies, waits for them, and re-layouts: 28.6 us -> 33.2 us
  waiting for transfers between devices: 41.6 us -> 38.6 us
  other arithmetic: 19.4 us -> 21.9 us
  matrix products: 57.8 us -> 60.1 us
  starting transfers between devices: 17.9 us -> 15.7 us
    ppermute x10, waiting for transfers between devices: 27.9 us -> 12.9 us  [swap(): return lax.ppermute(value, 'row', [(i, i ^ distance) for i in range(size)])]
    ppermute x6 -> x8, waiting for transfers between devices: 13.6 us -> 25.7 us  [col_sum(): lax.ppermute(value, 'col', [(i, i ^ distance) for i in range(size)])]
    dot_general x39, matrix products: 29.5 us -> 32.2 us  [dot_high(): jnp.dot(left, right, precision=lax.Precision.HIGHEST, preferred_element_t...]
    gather x2, local copies, waits for them, and re-layouts: 0.78 us -> 2.61 us  [shards(): jnp.take(gradient.reshape(-1, size, lanes), order, axis=1)]
    add x3 -> x4, other arithmetic: 3.07 us -> 4.66 us  [col_sum(): value + lax.ppermute(value, 'col', [(i, i ^ distance) for i in range(size)])]
    ppermute x6 -> x8, starting transfers between devices: 10.8 us -> 9.97 us  [col_sum(): lax.ppermute(value, 'col', [(i, i ^ distance) for i in range(size)])]
  transfers between devices with their start and end apart: 16 -> 18, of which waited for: 5 -> 7; matrix products, arithmetic and copies ran while one was open for 50% -> 60% of each run, Pallas kernels for 0% -> 0%
where the time goes in v4:
time: 175 us; the launch traced here: 171 us
  matrix products  60.1 us (34%)
  waiting for transfers between devices  38.6 us (22%)
  local copies, waits for them, and re-layouts  33.2 us (19%)
  other arithmetic  21.9 us (13%)
  starting transfers between devices  15.7 us (9%)
    dot_general x39, matrix products, dot_high(): jnp.dot(left, right, precision=lax.Precision.HIGHEST, preferred_element_t...  32.2 us
    ppermute x8, waiting for transfers between devices, col_sum(): lax.ppermute(value, 'col', [(i, i ^ distance) for i in range(size)])  25.7 us
    dot_general x2, matrix products, outer_mid(): jnp.einsum('rk,ck->rc', left, right, precision=lax.Precision.HIGH, prefer...  16.4 us
    ppermute x10, waiting for transfers between devices, swap(): return lax.ppermute(value, 'row', [(i, i ^ distance) for i in range(size)])  12.9 us
    ppermute x8, starting transfers between devices, col_sum(): lax.ppermute(value, 'col', [(i, i ^ distance) for i in range(size)])  9.97 us
    gather x1, local copies, waits for them, and re-layouts, shards(): jnp.take(held, jnp.arange(size) ^ me, axis=0).reshape(size * span, -1)  7.76 us
    another operation x1, other arithmetic, shards(): held = jnp.stack([held[key] for key in range(size)])  5.82 us
    dot_general x1, matrix products, inner_mid(): jnp.einsum('ra,rb->ab', left, right, precision=lax.Precision.HIGH, prefer...  5.81 us
  transfers between devices with their start and end apart: 18, of which 7 were waited for; matrix products, arithmetic and copies ran while one was open for 60% of the time, Pallas kernels for 0%

profile of v4, /device:TPU:0, one launch (start us, length us, event | category | flops | bytes accessed | tf_op | source)
XLA Modules:
  0.0 171.2 jit_solution(8035070449327981458)
XLA Ops:
  4.0 2.6 %collective-permute-start.1 = (f32[1,1024,512]{2,1,0:T(8,128)S(1)}, f32[1,1024,512]{2,1,0:T(8,128)}, u32[]{:S(2)}, u32[]{:S(2)}) collective-permute-start(f32[1,1024,512]{2,1,0:T(8,128)S(1)} %bitcast.92), channel_id=1, source_target_pairs={{0,8},{4,12},{8,0},{12,4},{1,9},{5,13},{9,1},{13,5},{2,10},{6,14},... | collective-permute-start | bytes 6291464 | tf_op jit(solution)/shard_map/ppermute | solution.py:114
  9.9 5.8 %fusion.185 = f32[512,4096]{1,0:T(8,128)S(1)} fusion(f32[256,512]{0,1:T(8,128)S(1)} %bitcast_select_fusion.2, f32[256,4096]{1,0:T(8,128)} %param.6), kind=kOutput, calls=%fused_computation.315 | convolution fusion | flops 3221225472 | bytes 13107200 | tf_op jit(solution)/shard_map/ra,rb->ab/dot_general | solution.py:42
  15.7 2.7 %slice.78 = f32[256,4096]{1,0:T(8,128)} slice(f32[512,4096]{1,0:T(8,128)S(1)} %fusion.185), slice={[0:256], [0:4096]} | slice | bytes 8388608 | tf_op jit(solution)/shard_map/slice | solution.py:180
  18.4 1.8 %copy-done = f32[512,4096]{1,0:T(8,128)} copy-done((f32[512,4096]{1,0:T(8,128)}, f32[512,4096]{1,0:T(8,128)S(1)}, u32[]{:S(2)}) %copy-start) | copy-done | bytes 8388632
  20.4 4.6 %fusion.184 = f32[512,512]{0,1:T(8,128)} fusion(f32[1024,512]{1,0:T(8,128)S(1)} %constant_dynamic-update-slice_fusion), kind=kOutput, calls=%fused_computation.314 | convolution fusion | flops 3221225472 | bytes 3145728 | tf_op jit(solution)/shard_map/ra,rb->ab/dot_general | solution.py:12
  25.6 3.6 %collective-permute-done.5 = f32[512,512]{0,1:T(8,128)} collective-permute-done((f32[512,512]{0,1:T(8,128)}, f32[512,512]{0,1:T(8,128)}, u32[]{:S(2)}, u32[]{:S(2)}) %collective-permute-start.5) | collective-permute-done | bytes 1048608 | tf_op jit(solution)/shard_map/ppermute | solution.py:114
  30.5 1.6 collective-permute-start.6
  32.6 3.2 %fusion.13 = f32[256,512]{1,0:T(8,128)S(1)} fusion(f32[1024,512]{1,0:T(8,128)S(1)} %constant_dynamic-update-slice_fusion, f32[256,4096]{1,0:T(8,128)} %param.6, s32[]{:T(128)S(6)} %select_n.477), kind=kOutput, calls=%fused_computation.40 | convolution fusion | flops 1610612736 | bytes 3670020 | tf_op jit(solution)/shard_map/dot_general | solution.py:8
  35.8 4.0 %collective-permute-done.6 = f32[256,256]{0,1:T(8,128)S(1)} collective-permute-done((f32[256,256]{0,1:T(8,128)S(1)}, f32[256,256]{0,1:T(8,128)S(1)}, u32[]{:S(2)}, u32[]{:S(2)}) %collective-permute-start.6) | collective-permute-done | bytes 262176 | tf_op jit(solution)/shard_map/ppermute | solution.py:141
  39.8 4.8 %collective-permute-done.8 = f32[256,256]{0,1:T(8,128)S(1)} collective-permute-done((f32[256,256]{0,1:T(8,128)S(1)}, f32[256,256]{0,1:T(8,128)S(1)}, u32[]{:S(2)}, u32[]{:S(2)}) %collective-permute-start.8) | collective-permute-done | bytes 262176 | tf_op jit(solution)/shard_map/ppermute | solution.py:141
  45.3 2.6 %collective-permute-start.7 = (f32[256,256]{0,1:T(8,128)}, f32[256,256]{0,1:T(8,128)}, u32[]{:S(2)}, u32[]{:S(2)}) collective-permute-start(f32[256,256]{0,1:T(8,128)} %get-tuple-element.18), channel_id=1, source_target_pairs={{0,2},{1,3},{2,0},{3,1},{4,6},{5,7},{6,4},{7,5},{8,10},{9,11},{10,... | collective-permute-start | bytes 786440 | tf_op jit(solution)/shard_map/ppermute | solution.py:141
  48.3 4.6 %collective-permute-done.1 = f32[1,1024,512]{2,1,0:T(8,128)} collective-permute-done((f32[1,1024,512]{2,1,0:T(8,128)S(1)}, f32[1,1024,512]{2,1,0:T(8,128)}, u32[]{:S(2)}, u32[]{:S(2)}) %collective-permute-start.1) | collective-permute-done | bytes 2097184 | tf_op jit(solution)/shard_map/ppermute | solution.py:114
  53.1 13.4 %collective-permute-done.7 = f32[256,256]{0,1:T(8,128)} collective-permute-done((f32[256,256]{0,1:T(8,128)}, f32[256,256]{0,1:T(8,128)}, u32[]{:S(2)}, u32[]{:S(2)}) %collective-permute-start.7) | collective-permute-done | bytes 262176 | tf_op jit(solution)/shard_map/ppermute | solution.py:141
  67.6 3.4 %collective-permute-done.9 = f32[256,256]{0,1:T(8,128)} collective-permute-done((f32[256,256]{0,1:T(8,128)S(1)}, f32[256,256]{0,1:T(8,128)}, u32[]{:S(2)}, u32[]{:S(2)}) %collective-permute-start.9) | collective-permute-done | bytes 262176 | tf_op jit(solution)/shard_map/ppermute | solution.py:141
  72.1 3.9 %convolution_add_fusion = f32[256,512]{1,0:T(8,128)S(1)} fusion(f32[256,512]{1,0:T(8,128)S(1)} %fusion.13, f32[1024,512]{1,0:T(8,128)} %collective-permute-done, f32[256,4096]{1,0:T(8,128)} %param.6, s32[]{:T(128)S(6)} %select_n.478), kind=kOutput, calls=%fused_computation.18 | convolution fusion | flops 1610743808 | bytes 4194308 | tf_op jit(solution)/shard_map/dot_general | solution.py:8
  76.0 3.5 %fusion.4 = f32[256,512]{1,0:T(8,128)S(1)} fusion(f32[256,512]{1,0:T(8,128)S(1)} %convolution_add_fusion, f32[1,1024,512]{2,1,0:T(8,128)} %collective-permute-done.1, f32[256,4096]{1,0:T(8,128)S(1)} %copy-done.1, s32[]{:T(128)S(6)} %select_n.479), kind=kOutput, calls=%fused_computation.16 | convolution fusion | flops 1610743808 | bytes 4194308 | tf_op jit(solution)/shard_map/dot_general | solution.py:8
  79.5 3.9 %slice_add_fusion = f32[256,4096]{1,0:T(8,128)S(1)} fusion(f32[256,4096]{1,0:T(8,128)} %collective-permute-done.10, f32[512,4096]{1,0:T(8,128)} %copy-done), kind=kLoop, calls=%fused_computation.10 | loop fusion | flops 1048576 | bytes 12582912 | tf_op jit(solution)/shard_map/add | solution.py:180
  84.2 4.5 %fusion.7 = f32[256,512]{1,0:T(8,128)S(1)} fusion(f32[256,512]{1,0:T(8,128)S(1)} %fusion.4, f32[1,1024,512]{2,1,0:T(8,128)} %collective-permute-done.2, f32[256,4096]{1,0:T(8,128)S(1)} %copy-done.1, s32[]{:T(128)S(6)} %select_n.480), kind=kOutput, calls=%fused_computation.17 | convolution fusion | flops 1610743808 | bytes 4194308 | tf_op jit(solution)/shard_map/dot_general | solution.py:8
  91.5 1.5 slice.55
  93.7 4.7 %collective-permute-done.11 = f32[256,512]{0,1:T(8,128)S(1)} collective-permute-done((f32[256,512]{0,1:T(8,128)S(1)}, f32[256,512]{0,1:T(8,128)S(1)}, u32[]{:S(2)}, u32[]{:S(2)}) %collective-permute-start.11) | collective-permute-done | bytes 524320 | tf_op jit(solution)/shard_map/ppermute | solution.py:114
  99.2 5.8 %pad_maximum_fusion = f32[4,1024,512]{2,1,0:T(8,128)} fusion(f32[1,1024,512]{2,1,0:T(8,128)} %collective-permute-done.2, f32[1,1024,512]{2,1,0:T(8,128)} %collective-permute-done.1, f32[1,1024,512]{2,1,0:T(8,128)} %bitcast.11, f32[1,1024,512]{2,1,0:T(8,128)S(1)} %bitcast.93), kind=kLoop, calls=%fused_computation.7 | loop fusion | flops 6291456 | bytes 16777216 | tf_op jit(solution)/shard_map/stack | solution.py:174
  105.0 7.8 %gather_fusion.6 = f32[4,1024,512]{2,1,0:T(8,128)} fusion(f32[4,1024,512]{2,1,0:T(8,128)} %pad_maximum_fusion, s32[1024]{0:T(1024)S(1)} %pad_clamp_fusion), kind=kCustom, calls=%fused_computation.6 | custom fusion | bytes 16777232 | tf_op jit(solution)/shard_map/jit(_take)/gather | solution.py:206
  113.5 1.8 %slice_add_fusion.6 = (f32[256,256]{1,0:T(8,128)S(1)}, f32[256,256]{1,0:T(8,128)}) fusion(f32[256,256]{1,0:T(8,128)} %copy-done.6, f32[256,512]{1,0:T(8,128)S(1)} %fusion.7, f32[256,256]{1,0:T(8,128)} %collective-permute-done.3), kind=kLoop, calls=%fused_computation.307 | loop fusion | flops 131072 | bytes 1572864 | tf_op jit(solution)/shard_map/add | solution.py:141
  115.3 2.9 %collective-permute-start.14 = (f32[256,256]{1,0:T(8,128)S(1)}, f32[256,256]{1,0:T(8,128)S(1)}, u32[]{:S(2)}, u32[]{:S(2)}) collective-permute-start(f32[256,256]{1,0:T(8,128)S(1)} %get-tuple-element.14), channel_id=1, source_target_pairs={{0,2},{1,3},{2,0},{3,1},{4,6},{5,7},{6,4},{7,5},{8,10},{9,11},{10,... | collective-permute-start | bytes 786440 | tf_op jit(solution)/shard_map/ppermute | solution.py:141
  122.9 2.3 %gather_fusion.2 = f32[256]{0:T(256)S(1)} fusion(f32[256,256]{1,0:T(8,128)S(1)} %get-tuple-element.12, s32[256]{0:T(256)S(1)} %bitcast.88), kind=kCustom, calls=%fused_computation.2 | custom fusion | bytes 4096 | tf_op jit(solution)/shard_map/jit(_diag)/jit(diagonal)/cond/branch_0_fun/gather | solution.py:99
  125.2 2.3 %gather_fusion.4 = f32[256]{0:T(256)S(1)} fusion(f32[256,256]{1,0:T(8,128)S(1)} %get-tuple-element.13, s32[256]{0:T(256)S(1)} %bitcast.89), kind=kCustom, calls=%fused_computation.4 | custom fusion | bytes 4096 | tf_op jit(solution)/shard_map/jit(_diag)/jit(diagonal)/cond/branch_0_fun/gather | solution.py:99
  127.7 2.3 %gather_fusion.3 = f32[256]{0:T(256)S(1)} fusion(f32[256,256]{1,0:T(8,128)S(1)} %get-tuple-element.10, s32[256]{0:T(256)S(1)} %bitcast.90), kind=kCustom, calls=%fused_computation.3 | custom fusion | bytes 4096 | tf_op jit(solution)/shard_map/jit(_diag)/jit(diagonal)/cond/branch_0_fun/gather | solution.py:102
  137.2 2.7 %gather_fusion.5 = f32[256]{0:T(256)S(1)} fusion(f32[256,256]{1,0:T(8,128)S(1)} %get-tuple-element.11, s32[256]{0:T(256)S(1)} %bitcast.91), kind=kCustom, calls=%fused_computation.5 | custom fusion | bytes 4096 | tf_op jit(solution)/shard_map/jit(_diag)/jit(diagonal)/cond/branch_0_fun/gather | solution.py:102
  146.7 2.0 %fusion.58 = f32[256,256]{0,1:T(8,128)S(1)} fusion(f32[256,256]{1,0:T(8,128)S(1)} %convolution_subtract_fusion.9, f32[256,256]{1,0:T(8,128)} %get-tuple-element.15, f32[256,256]{1,0:T(8,128)} %collective-permute-done.4), kind=kOutput, calls=%fused_computation.95 | convolution fusion | flops 201392128 | bytes 1048576 | tf_op jit(solution)/shard_map/dot_general | solution.py:8
  151.5 2.2 %bitcast_select_fusion = f32[4096,512]{1,0:T(8,128)S(1)} fusion(f32[4,1024,512]{2,1,0:T(8,128)S(1)} %bitcast.95, pred[4096]{0:T(1024)(128)(4,1)S(1)} %bitcast.98), kind=kLoop, calls=%fused_computation.8 | loop fusion | flops 2097152 | bytes 16781312 | tf_op jit(solution)/shard_map/jit(_take)/select_n | solution.py:206
  154.6 8.9 %convolution_subtract_fusion = f32[256,4096]{1,0:T(8,128)} fusion(f32[256,4096]{1,0:T(8,128)S(1)} %copy-done.2, f32[4096,512]{1,0:T(8,128)S(1)} %bitcast_select_fusion, f32[256,256]{0,1:T(8,128)S(1)} %fusion.40, f32[256,256]{0,1:T(8,128)S(1)} %fusion.58), kind=kOutput, calls=%fused_computation.9 | convolution fusion | flops 3222405120 | bytes 17301504 | tf_op jit(solution)/shard_map/rk,ck->rc/dot_general | solution.py:32
  163.5 7.5 %add_subtract_fusion = f32[128,4096]{1,0:T(8,128)} fusion(f32[128,4096]{1,0:T(8,128)} %collective-permute-done.15, f32[256,4096]{1,0:T(8,128)S(1)} %copy-done.4, f32[4096,512]{1,0:T(8,128)S(1)} %bitcast_select_fusion, f32[128,512]{1,0:T(8,128)S(1)} %collective-permute-done.17, f32[256,512]{1,0:T(8,128)S(1)} %slice_add_fusion.1), kind=kOutput, calls=%fused_computation.15 | convolution fusion | flops 1611726848 | bytes 15204352 | tf_op jit(solution)/shard_map/rk,ck->rc/dot_general | solution.py:32
  (131 shorter events, 40.1 us)
Async XLA Ops:
  0.6 6.0 %copy-start.7 = (s32[4]{0:T(128)S(1)}, s32[4]{0:T(128)}, u32[]{:S(2)}) copy-start(s32[4]{0:T(128)} %constant.382.clone) | copy-start | bytes 52
  0.6 6.0 %copy-start.5 = (f32[256,512]{1,0:T(8,128)S(1)}, f32[256,512]{1,0:T(8,128)}, u32[]{:S(2)}) copy-start(f32[256,512]{1,0:T(8,128)} %param.9) | copy-start | bytes 1572868
  3.5 68.6 %collective-permute-start = (f32[1024,512]{1,0:T(8,128)S(1)}, f32[1024,512]{1,0:T(8,128)}, u32[]{:S(2)}, u32[]{:S(2)}) collective-permute-start(f32[1024,512]{1,0:T(8,128)S(1)} %constant_dynamic-update-slice_fusion), channel_id=1, source_target_pairs={{0,4},{4,0},{8,12},{12,8},{1,5},{5,1},{9,13},{13,9},{2,6},{6,2},{1... | collective-permute-start | bytes 6291464 | tf_op jit(solution)/shard_map/ppermute | solution.py:114
  4.0 48.9 %collective-permute-start.1 = (f32[1,1024,512]{2,1,0:T(8,128)S(1)}, f32[1,1024,512]{2,1,0:T(8,128)}, u32[]{:S(2)}, u32[]{:S(2)}) collective-permute-start(f32[1,1024,512]{2,1,0:T(8,128)S(1)} %bitcast.92), channel_id=1, source_target_pairs={{0,8},{4,12},{8,0},{12,4},{1,9},{5,13},{9,1},{13,5},{2,10},{6,14},... | collective-permute-start | bytes 6291464 | tf_op jit(solution)/shard_map/ppermute | solution.py:114
  15.7 4.5 %copy-start = (f32[512,4096]{1,0:T(8,128)}, f32[512,4096]{1,0:T(8,128)S(1)}, u32[]{:S(2)}) copy-start(f32[512,4096]{1,0:T(8,128)S(1)} %fusion.185) | copy-start | bytes 25165828
  20.2 59.3 %collective-permute-start.10 = (f32[256,4096]{1,0:T(8,128)}, f32[256,4096]{1,0:T(8,128)}, u32[]{:S(2)}, u32[]{:S(2)}) collective-permute-start(f32[256,4096]{1,0:T(8,128)} %slice.78), channel_id=1, source_target_pairs={{0,4},{4,0},{8,12},{12,8},{1,5},{5,1},{9,13},{13,9},{2,6},{6,2},{1... | collective-permute-start | bytes 12582920 | tf_op jit(solution)/shard_map/ppermute | solution.py:114
  25.0 4.2 %collective-permute-start.5 = (f32[512,512]{0,1:T(8,128)}, f32[512,512]{0,1:T(8,128)}, u32[]{:S(2)}, u32[]{:S(2)}) collective-permute-start(f32[512,512]{0,1:T(8,128)} %fusion.184), channel_id=1, source_target_pairs={{0,4},{4,0},{8,12},{12,8},{1,5},{5,1},{9,13},{13,9},{2,6},{6,2},{1... | collective-permute-start | bytes 3145736 | tf_op jit(solution)/shard_map/ppermute | solution.py:114
  30.5 9.2 %collective-permute-start.6 = (f32[256,256]{0,1:T(8,128)S(1)}, f32[256,256]{0,1:T(8,128)S(1)}, u32[]{:S(2)}, u32[]{:S(2)}) collective-permute-start(f32[256,256]{0,1:T(8,128)S(1)} %get-tuple-element.20), channel_id=1, source_target_pairs={{0,1},{1,0},{2,3},{3,2},{4,5},{5,4},{6,7},{7,6},{8,9},{9,8},{10,11... | collective-permute-start | bytes 786440 | tf_op jit(solution)/shard_map/ppermute | solution.py:141
  32.2 12.4 %collective-permute-start.8 = (f32[256,256]{0,1:T(8,128)S(1)}, f32[256,256]{0,1:T(8,128)S(1)}, u32[]{:S(2)}, u32[]{:S(2)}) collective-permute-start(f32[256,256]{0,1:T(8,128)S(1)} %get-tuple-element.21), channel_id=1, source_target_pairs={{0,1},{1,0},{2,3},{3,2},{4,5},{5,4},{6,7},{7,6},{8,9},{9,8},{10,11... | collective-permute-start | bytes 786440 | tf_op jit(solution)/shard_map/ppermute | solution.py:141
  45.3 21.2 %collective-permute-start.7 = (f32[256,256]{0,1:T(8,128)}, f32[256,256]{0,1:T(8,128)}, u32[]{:S(2)}, u32[]{:S(2)}) collective-permute-start(f32[256,256]{0,1:T(8,128)} %get-tuple-element.18), channel_id=1, source_target_pairs={{0,2},{1,3},{2,0},{3,1},{4,6},{5,7},{6,4},{7,5},{8,10},{9,11},{10,... | collective-permute-start | bytes 786440 | tf_op jit(solution)/shard_map/ppermute | solution.py:141
  47.9 23.1 %collective-permute-start.9 = (f32[256,256]{0,1:T(8,128)S(1)}, f32[256,256]{0,1:T(8,128)}, u32[]{:S(2)}, u32[]{:S(2)}) collective-permute-start(f32[256,256]{0,1:T(8,128)S(1)} %get-tuple-element.19), channel_id=1, source_target_pairs={{0,2},{1,3},{2,0},{3,1},{4,6},{5,7},{6,4},{7,5},{8,10},{9,11},{10,... | collective-permute-start | bytes 786440 | tf_op jit(solution)/shard_map/ppermute | solution.py:141
  52.9 31.3 %collective-permute-start.2 = (f32[1,1024,512]{2,1,0:T(8,128)}, f32[1,1024,512]{2,1,0:T(8,128)}, u32[]{:S(2)}, u32[]{:S(2)}) collective-permute-start(f32[1,1024,512]{2,1,0:T(8,128)} %collective-permute-done.1), channel_id=1, source_target_pairs={{0,4},{4,0},{8,12},{12,8},{1,5},{5,1},{9,13},{13,9},{2,6},{6,2},{1... | collective-permute-start | bytes 6291464 | tf_op jit(solution)/shard_map/ppermute | solution.py:114
  53.0 22.9 %copy-start.1 = (f32[256,4096]{1,0:T(8,128)S(1)}, f32[256,4096]{1,0:T(8,128)}, u32[]{:S(2)}) copy-start(f32[256,4096]{1,0:T(8,128)} %param.6) | copy-start | bytes 12582916
  83.5 9.6 %copy-start.3 = (f32[256,4096]{1,0:T(8,128)}, f32[256,4096]{1,0:T(8,128)S(1)}, u32[]{:S(2)}) copy-start(f32[256,4096]{1,0:T(8,128)S(1)} %slice_add_fusion) | copy-start | bytes 12582916
  83.5 14.9 %collective-permute-start.11 = (f32[256,512]{0,1:T(8,128)S(1)}, f32[256,512]{0,1:T(8,128)S(1)}, u32[]{:S(2)}, u32[]{:S(2)}) collective-permute-start(f32[256,512]{0,1:T(8,128)S(1)} %pad_maximum_fusion.2), channel_id=1, source_target_pairs={{0,8},{4,12},{8,0},{12,4},{1,9},{5,13},{9,1},{13,5},{2,10},{6,14},... | collective-permute-start | bytes 1572872 | tf_op jit(solution)/shard_map/ppermute | solution.py:114
  89.5 23.3 %collective-permute-start.13 = (f32[256,256]{1,0:T(8,128)}, f32[256,256]{1,0:T(8,128)S(1)}, u32[]{:S(2)}, u32[]{:S(2)}) collective-permute-start(f32[256,256]{1,0:T(8,128)} %get-tuple-element.16), channel_id=1, source_target_pairs={{0,1},{1,0},{2,3},{3,2},{4,5},{5,4},{6,7},{7,6},{8,9},{9,8},{10,11... | collective-permute-start | bytes 786440 | tf_op jit(solution)/shard_map/ppermute | solution.py:141
  90.1 23.4 %collective-permute-start.3 = (f32[256,256]{1,0:T(8,128)}, f32[256,256]{1,0:T(8,128)}, u32[]{:S(2)}, u32[]{:S(2)}) collective-permute-start(f32[256,256]{1,0:T(8,128)} %get-tuple-element.17), channel_id=1, source_target_pairs={{0,1},{1,0},{2,3},{3,2},{4,5},{5,4},{6,7},{7,6},{8,9},{9,8},{10,11... | collective-permute-start | bytes 786440 | tf_op jit(solution)/shard_map/ppermute | solution.py:141
  93.0 70.5 %collective-permute-start.15 = (f32[128,4096]{1,0:T(8,128)}, f32[128,4096]{1,0:T(8,128)}, u32[]{:S(2)}, u32[]{:S(2)}) collective-permute-start(f32[128,4096]{1,0:T(8,128)} %slice.55), channel_id=1, source_target_pairs={{0,8},{4,12},{8,0},{12,4},{1,9},{5,13},{9,1},{13,5},{2,10},{6,14},... | collective-permute-start | bytes 6291464 | tf_op jit(solution)/shard_map/ppermute | solution.py:114
  99.2 19.1 %collective-permute-start.12 = (f32[256,512]{0,1:T(8,128)}, f32[256,512]{0,1:T(8,128)}, u32[]{:S(2)}, u32[]{:S(2)}) collective-permute-start(f32[256,512]{0,1:T(8,128)} %add.377), channel_id=1, source_target_pairs={{0,4},{4,0},{8,12},{12,8},{1,5},{5,1},{9,13},{13,9},{2,6},{6,2},{1... | collective-permute-start | bytes 1572872 | tf_op jit(solution)/shard_map/ppermute | solution.py:114
  112.8 0.7 copy-start.6
  115.3 31.4 %collective-permute-start.4 = (f32[256,256]{1,0:T(8,128)}, f32[256,256]{1,0:T(8,128)}, u32[]{:S(2)}, u32[]{:S(2)}) collective-permute-start(f32[256,256]{1,0:T(8,128)} %get-tuple-element.15), channel_id=1, source_target_pairs={{0,2},{1,3},{2,0},{3,1},{4,6},{5,7},{6,4},{7,5},{8,10},{9,11},{10,... | collective-permute-start | bytes 786440 | tf_op jit(solution)/shard_map/ppermute | solution.py:141
  115.3 34.4 %collective-permute-start.14 = (f32[256,256]{1,0:T(8,128)S(1)}, f32[256,256]{1,0:T(8,128)S(1)}, u32[]{:S(2)}, u32[]{:S(2)}) collective-permute-start(f32[256,256]{1,0:T(8,128)S(1)} %get-tuple-element.14), channel_id=1, source_target_pairs={{0,2},{1,3},{2,0},{3,1},{4,6},{5,7},{6,4},{7,5},{8,10},{9,11},{10,... | collective-permute-start | bytes 786440 | tf_op jit(solution)/shard_map/ppermute | solution.py:141
  141.7 9.7 %slice-start = ((s8[8388608]{0:T(1024)(128)(4,1)}), s8[4194304]{0:T(1024)(128)(4,1)S(1)}, s32[]{:S(2)}) async-start(s8[8388608]{0:T(1024)(128)(4,1)} %bitcast.94), calls=%async_computation | async-start | bytes 8388608
  145.8 5.7 %slice-start.1 = ((s8[8388608]{0:T(1024)(128)(4,1)}), s8[4194304]{0:T(1024)(128)(4,1)S(1)}, s32[]{:S(2)}) async-start(s8[8388608]{0:T(1024)(128)(4,1)} %bitcast.94), calls=%async_computation.1 | async-start | bytes 8388608
  151.4 2.3 %collective-permute-start.16 = (f32[256,512]{1,0:T(8,128)S(1)}, f32[256,512]{1,0:T(8,128)S(1)}, u32[]{:S(2)}, u32[]{:S(2)}) collective-permute-start(f32[256,512]{1,0:T(8,128)S(1)} %slice.84), channel_id=1, source_target_pairs={{0,4},{4,0},{8,12},{12,8},{1,5},{5,1},{9,13},{13,9},{2,6},{6,2},{1... | collective-permute-start | bytes 1572872 | tf_op jit(solution)/shard_map/ppermute | solution.py:114
  151.5 3.1 %copy-start.2 = (f32[256,4096]{1,0:T(8,128)S(1)}, f32[256,4096]{1,0:T(8,128)}, u32[]{:S(2)}) copy-start(f32[256,4096]{1,0:T(8,128)} %param.6) | copy-start | bytes 12582916
  153.8 9.7 %copy-start.4 = (f32[256,4096]{1,0:T(8,128)S(1)}, f32[256,4096]{1,0:T(8,128)}, u32[]{:S(2)}) copy-start(f32[256,4096]{1,0:T(8,128)} %copy-done.3) | copy-start | bytes 12582916
  153.9 9.7 %collective-permute-start.17 = (f32[128,512]{1,0:T(8,128)S(1)}, f32[128,512]{1,0:T(8,128)S(1)}, u32[]{:S(2)}, u32[]{:S(2)}) collective-permute-start(f32[128,512]{1,0:T(8,128)S(1)} %slice.86), channel_id=1, source_target_pairs={{0,8},{4,12},{8,0},{12,4},{1,9},{5,13},{9,1},{13,5},{2,10},{6,14},... | collective-permute-start | bytes 786440 | tf_op jit(solution)/shard_map/ppermute | solution.py:114
